TPU v7x, 256 devices: a whole 4x4x8 slice. The times are simulated.
256 devices in a mesh: pix: 32 (over z, x), feat: 8 (over y, core).
Axes of the slice: x: 4, y: 4, z: 8, core: 2. Of those that a mesh axis runs over, the one named last changes fastest.
Arguments:
- mass_bin: int32 [262144, 256], P(('pix', 'feat')), may hold values from 0 to 255
- mobility_bin: int32 [262144, 256], P(('pix', 'feat')), may hold values from 0 to 15
- intensity: bfloat16 [262144, 256], P(('pix', 'feat')), may hold values from 10 to 4000, as said below
- basis_init: float32 [262144, 64], P(('pix', 'feat')), may hold values from 0.1 to 1
- profile_init: float32 [64, 4096], P(None, 'feat'), may hold values from 0.1 to 1
Outputs:
- basis: float32 [262144, 64], P(('pix', 'feat'))
- profiles: float32 [64, 4096], P(None, 'feat')
Inputs may be any that keep to these rules, and one draw needn't show every extreme that they name: `intensity`: positive peak intensities.
All inputs are finite; a program needn't handle non-finite values.
Results may differ from a plain program's by a relative error of at most 0.00045.
Values may be sent and summed in bfloat16 or wider, within the bound.
No kernel may reach another device: no remote copies, remote signals or barrier semaphores. Data moves between devices by JAX's collectives and lax.ppermute only.
A program may use at most 64 MiB of HBM per device.

v0:
```python
import math

import jax
import jax.numpy as jnp
from jax import lax
from jax.sharding import PartitionSpec as P

MZ = 256
MOB = 16
PEAKS = 256
ITERS = 2


EPS = 1e-06


def bin_block(args):
    mass, mobility, weight = args
    mass_hot = (mass[:, :, None] == jnp.arange(MZ, dtype=jnp.int32)[None, None, :]).astype(
        jnp.bfloat16
    ) * weight[:, :, None]
    mobility_hot = (mobility[:, :, None] == jnp.arange(MOB, dtype=jnp.int32)[None, None, :]).astype(
        jnp.bfloat16
    )
    dense = jnp.einsum("pkb,pkm->pbm", mobility_hot, mass_hot, preferred_element_type=jnp.float32)
    return dense.reshape(mass.shape[0], MZ * MOB).astype(jnp.bfloat16)


def local(mass_bin, mobility_bin, intensity, basis_init, profile_init):
    rows = mass_bin.shape[0]
    block = math.gcd(rows, 32)
    count = rows // block
    spectra = lax.map(
        bin_block,
        (
            mass_bin.reshape(count, block, PEAKS),
            mobility_bin.reshape(count, block, PEAKS),
            intensity.reshape(count, block, PEAKS),
        ),
    )
    spectra = spectra.reshape(rows, MZ * MOB)
    highest = lax.Precision.HIGHEST
    basis, profiles = (basis_init, profile_init)
    for step in range(ITERS):
        partial_h = lax.dot_general(
            basis.astype(jnp.bfloat16),
            spectra,
            (((0,), (0,)), ((), ())),
            preferred_element_type=jnp.float32,
        )
        partial_gram = lax.dot_general(
            basis,
            basis,
            (((0,), (0,)), ((), ())),
            precision=highest,
            preferred_element_type=jnp.float32,
        )
        shared = lax.psum_scatter(partial_h, "feat", scatter_dimension=1, tiled=True)
        numer_h = lax.psum(shared, "pix")
        gram_w = lax.psum(partial_gram, ("pix", "feat"))
        profiles = (
            profiles
            * numer_h
            / (
                jnp.dot(gram_w, profiles, precision=highest, preferred_element_type=jnp.float32)
                + EPS
            )
        )
        numer_w = lax.dot_general(
            spectra,
            lax.all_gather(profiles.astype(jnp.bfloat16), "feat", axis=1, tiled=True),
            (((1,), (1,)), ((), ())),
            preferred_element_type=jnp.float32,
        )
        local_gram = lax.dot_general(
            profiles,
            profiles,
            (((1,), (1,)), ((), ())),
            precision=highest,
            preferred_element_type=jnp.float32,
        )
        gram_h = lax.psum(local_gram, "feat")
        basis = (
            basis
            * numer_w
            / (jnp.dot(basis, gram_h, precision=highest, preferred_element_type=jnp.float32) + EPS)
        )
    return (basis, profiles)


def solution(mesh):
    return jax.shard_map(
        local,
        mesh=mesh,
        in_specs=(
            P(("pix", "feat"), None),
            P(("pix", "feat"), None),
            P(("pix", "feat"), None),
            P(("pix", "feat"), None),
            P(None, "feat"),
        ),
        out_specs=(P(("pix", "feat"), None), P(None, "feat")),
        check_vma=False,
    )
```

profile of v0, /device:TPU:16, one launch (start us, length us, event | category | flops | bytes accessed | tf_op | source)
XLA Modules:
  0.0 662.2 jit_solution(15157433333801755827)
XLA Ops:
  7.2 192.9 %while.10 = (s32[]{:T(128)}, bf16[32,32,4096]{2,1,0:T(8,128)(2,1)}, s32[32,32,256]{2,1,0:T(8,128)}, s32[32,32,256]{2,1,0:T(8,128)}, bf16[32,32,256]{2,1,0:T(8,128)(2,1)}, /*index=5*/s32[]{:T(128)}) while((s32[]{:T(128)}, bf16[32,32,4096]{2,1,0:T(8,128)(2,1)}, s32[32,32,256]{2,1,0:T(8,128)}, s32[32,32,256]{2,1,0:T(8,128)}, ...), condition=%wide.region_1.2_spmd, body=%wide.region_0.1_spmd.sunk | while | flops 71565312 | bytes 1557069 | solution.py:33
  7.2 0.8 dynamic-slice_bitcast_fusion.5
  8.8 3.7 fusion.50
  13.3 0.8 dynamic-slice_bitcast_fusion.5
  14.8 3.7 fusion.50
  19.3 0.8 dynamic-slice_bitcast_fusion.5
  20.8 3.7 fusion.50
  25.3 0.8 dynamic-slice_bitcast_fusion.5
  26.8 3.7 fusion.50
  31.4 0.8 dynamic-slice_bitcast_fusion.5
  32.9 3.7 fusion.50
  37.4 0.8 dynamic-slice_bitcast_fusion.5
  38.9 3.7 fusion.50
  43.4 0.8 dynamic-slice_bitcast_fusion.5
  44.9 3.7 fusion.50
  49.5 0.8 dynamic-slice_bitcast_fusion.5
  51.0 3.7 fusion.50
  55.5 0.8 dynamic-slice_bitcast_fusion.5
  57.0 3.7 fusion.50
  61.5 0.8 dynamic-slice_bitcast_fusion.5
  63.0 3.7 fusion.50
  67.5 0.8 dynamic-slice_bitcast_fusion.5
  69.0 3.7 fusion.50
  73.6 0.8 dynamic-slice_bitcast_fusion.5
  75.1 3.7 fusion.50
  79.6 0.8 dynamic-slice_bitcast_fusion.5
  81.1 3.7 fusion.50
  87.1 3.7 fusion.50
  93.2 3.7 fusion.50
  97.7 0.8 dynamic-slice_bitcast_fusion.5
  99.2 3.7 fusion.50
  105.2 3.7 fusion.50
  111.2 3.7 fusion.50
  117.2 3.7 fusion.50
  123.3 3.7 fusion.50
  129.3 3.7 fusion.50
  135.3 3.7 fusion.50
  141.4 3.7 fusion.50
  147.4 3.7 fusion.50
  153.4 3.7 fusion.50
  159.4 3.7 fusion.50
  165.5 3.7 fusion.50
  171.5 3.7 fusion.50
  177.5 3.7 fusion.50
  183.6 3.7 fusion.50
  189.6 3.7 fusion.50
  195.6 3.7 fusion.50
  200.1 6.1 convolution_bitcast_fusion
  206.2 32.3 %reduce-scatter.3.cloned.1.call-done = f32[64,512]{1,0:T(8,128)} async-done(((f32[64,4096]{1,0:T(8,128)}), f32[64,512]{1,0:T(8,128)}) %reduce-scatter.3.cloned.1.call-update) | async-done | bytes 131088 | tf_op jit(solution)/shard_map/reduce_scatter | solution.py:58
  239.0 79.6 %psum.43 = f32[64,64]{1,0:T(8,128)S(1)} all-reduce(f32[64,64]{1,0:T(8,128)S(1)} %fusion.21), channel_id=1, replica_groups=mesh['pix'=32,'feat'=8] {'pix','feat'}, use_global_device_ids=true, to_apply=%region_4.5 | all-reduce | flops 4096 | bytes 32768 | tf_op jit(solution)/shard_map/psum | solution.py:60
  318.6 68.1 %all-reduce.3.cloned.1.call-done = f32[64,512]{1,0:T(8,128)} async-done(((f32[64,512]{1,0:T(8,128)}), f32[64,512]{1,0:T(8,128)}) %all-reduce.3.cloned.1.call-update) | async-done | bytes 131088 | tf_op jit(solution)/shard_map/psum | solution.py:59
  386.7 1.2 fusion.19
  387.9 11.9 %all_gather.6 = bf16[64,4096]{1,0:T(8,128)(2,1)S(1)} all-gather(bf16[64,512]{1,0:T(8,128)(2,1)S(1)} %get-tuple-element.42), channel_id=1, replica_groups=mesh['pix'=32,'feat'=8] {'feat'}, dimensions={1}, use_global_device_ids=true | all-gather | bytes 589824 | tf_op jit(solution)/shard_map/all_gather | solution.py:71
  399.8 6.0 convolution_multiply_fusion.1
  406.1 21.5 %psum.44 = f32[64,64]{1,0:T(8,128)S(1)} all-reduce(f32[64,64]{1,0:T(8,128)S(1)} %fusion.22), channel_id=1, replica_groups=mesh['pix'=32,'feat'=8] {'feat'}, use_global_device_ids=true, to_apply=%region_5.6 | all-reduce | flops 4096 | bytes 32768 | tf_op jit(solution)/shard_map/psum | solution.py:82
  428.0 6.0 fusion.16
  434.1 31.3 %reduce-scatter.5.cloned.1.call-done = f32[64,512]{1,0:T(8,128)} async-done(((f32[64,4096]{1,0:T(8,128)}), f32[64,512]{1,0:T(8,128)}) %reduce-scatter.5.cloned.1.call-update) | async-done | bytes 131088 | tf_op jit(solution)/shard_map/reduce_scatter | solution.py:58
  465.7 79.5 %psum.46 = f32[64,64]{1,0:T(8,128)S(1)} all-reduce(f32[64,64]{1,0:T(8,128)S(1)} %fusion.23), channel_id=1, replica_groups=mesh['pix'=32,'feat'=8] {'pix','feat'}, use_global_device_ids=true, to_apply=%region_8.9 | all-reduce | flops 4096 | bytes 32768 | tf_op jit(solution)/shard_map/psum | solution.py:60
  545.2 68.5 %all-reduce.5.cloned.1.call-done = f32[64,512]{1,0:T(8,128)} async-done(((f32[64,512]{1,0:T(8,128)}), f32[64,512]{1,0:T(8,128)}) %all-reduce.5.cloned.1.call-update) | async-done | bytes 131088 | tf_op jit(solution)/shard_map/psum | solution.py:59
  613.7 1.2 fusion.20
  614.9 11.9 %all_gather.7 = bf16[64,4096]{1,0:T(8,128)(2,1)S(1)} all-gather(bf16[64,512]{1,0:T(8,128)(2,1)S(1)} %get-tuple-element.44), channel_id=1, replica_groups=mesh['pix'=32,'feat'=8] {'feat'}, dimensions={1}, use_global_device_ids=true | all-gather | bytes 589824 | tf_op jit(solution)/shard_map/all_gather | solution.py:71
  626.8 6.0 convolution_multiply_fusion
  633.1 21.5 %psum.47 = f32[64,64]{1,0:T(8,128)S(1)} all-reduce(f32[64,64]{1,0:T(8,128)S(1)} %fusion.24), channel_id=1, replica_groups=mesh['pix'=32,'feat'=8] {'feat'}, use_global_device_ids=true, to_apply=%region_9.10 | all-reduce | flops 4096 | bytes 32768 | tf_op jit(solution)/shard_map/psum | solution.py:82
  654.6 1.1 fusion.11
  (134 shorter events, 66.4 us)
Async XLA Ops:
  7.2 231.4 %reduce-scatter.3.cloned.1.call-start = ((), (), s32[]{:S(2)}) async-start(), calls=%async_computation.2 | async-start | bytes 1179648 | tf_op jit(solution)/shard_map/reduce_scatter | solution.py:58
  7.2 192.9 %copy-start = (f32[1024,64]{0,1:T(8,128)S(1)}, f32[1024,64]{0,1:T(8,128)}, u32[]{:S(2)}) copy-start(f32[1024,64]{0,1:T(8,128)} %param.10) | copy-start | bytes 786436
  200.1 186.6 %copy-start.2 = (f32[64,512]{1,0:T(8,128)S(1)}, f32[64,512]{1,0:T(8,128)}, u32[]{:S(2)}) copy-start(f32[64,512]{1,0:T(8,128)} %param.11) | copy-start | bytes 393220
  206.2 180.5 %all-reduce.3.cloned.1.call-start = ((), (), s32[]{:S(2)}) async-start(), calls=%async_computation.3 | async-start | bytes 262144 | tf_op jit(solution)/shard_map/psum | solution.py:59
  238.6 226.7 %reduce-scatter.5.cloned.1.call-start = ((), (), s32[]{:S(2)}) async-start(), calls=%async_computation.4 | async-start | bytes 1179648 | tf_op jit(solution)/shard_map/reduce_scatter | solution.py:58
  434.0 179.7 %all-reduce.5.cloned.1.call-start = ((), (), s32[]{:S(2)}) async-start(), calls=%async_computation.5 | async-start | bytes 262144 | tf_op jit(solution)/shard_map/psum | solution.py:59
  614.9 40.8 %copy-start.1 = (f32[64,512]{1,0:T(8,128)}, f32[64,512]{1,0:T(8,128)S(1)}, u32[]{:S(2)}) copy-start(f32[64,512]{1,0:T(8,128)S(1)} %get-tuple-element.45) | copy-start | bytes 393220
Sparse Core Ops, SparseCore 0:
  206.3 32.2 reduce-scatter.2
  242.0 144.5 all-reduce.2
  434.1 31.1 reduce-scatter.4
  469.0 144.6 all-reduce.4
where the time goes:
time: 673 us; the launch traced here: 662 us
  blocking collectives  226 us (34%)
  waiting for transfers between devices  200 us (30%)
  matrix products  146 us (22%)
  local copies, waits for them, and re-layouts  75.5 us (11%)
  between operations  13.9 us (2%)
    psum x2, blocking collectives, local(): gram_w = lax.psum(partial_gram, ('pix', 'feat'))  159 us
    psum x2, waiting for transfers between devices, local(): numer_h = lax.psum(shared, 'pix')  137 us
    dot_general x32, matrix products, bin_block(): jnp.einsum('pkb,pkm->pbm', mobility_hot, mass_hot, preferred_element_type...  117 us
    reduce_scatter x2, waiting for transfers between devices, local(): lax.psum_scatter(partial_h, 'feat', scatter_dimension=1, tiled=True)  63.6 us
    psum x2, blocking collectives, local(): gram_h = lax.psum(local_gram, 'feat')  42.9 us
    eq x32, local copies, waits for them, and re-layouts, bin_block(): mass[:, :, None] == jnp.arange(MZ, dtype=jnp.int32)[None, None, :]  25 us
    all_gather x2, blocking collectives, local(): lax.all_gather(profiles.astype(jnp.bfloat16), 'feat', axis=1, tiled=True)  23.8 us
    dynamic_update_slice x32, local copies, waits for them, and re-layouts, local(): lax.map(bin_block, (mass_bin.reshape(count, block, PEAKS), mobility_bin.r...  23.4 us
  transfers between devices with their start and end apart: 4, of which 4 were waited for; matrix products, arithmetic and copies ran while one was open for 0% of the time, Pallas kernels for 0%

commit v1 on v0

--- a/solution.py
+++ b/solution.py
@@ -26,7 +26,48 @@
     return dense.reshape(mass.shape[0], MZ * MOB).astype(jnp.bfloat16)
 
 
+def pairs(n, s):
+    return [(i, i ^ s) for i in range(n)]
+
+
+def halve_scatter(x, g, axis, n):
+    j = lax.axis_index(axis)
+    s = n // 2
+    while s >= 1:
+        half = x.shape[1] // 2
+        bit = (j // s) % 2
+        keep = lax.dynamic_slice_in_dim(x, bit * half, half, axis=1)
+        send = lax.dynamic_slice_in_dim(x, (1 - bit) * half, half, axis=1)
+        got = lax.ppermute(jnp.concatenate([send, g], axis=1), axis, pairs(n, s))
+        x = keep + got[:, :half]
+        g = g + got[:, half:]
+        s //= 2
+    return x, g
+
+
+def double_sum(x, axis, n):
+    s = 1
+    while s < n:
+        x = x + lax.ppermute(x, axis, pairs(n, s))
+        s *= 2
+    return x
+
+
+def double_gather(x, g, axis, n):
+    j = lax.axis_index(axis)
+    s = 1
+    while s < n:
+        other, got_g = lax.ppermute((x, g), axis, pairs(n, s))
+        bit = (j // s) % 2
+        x = jnp.where(bit == 1, jnp.concatenate([other, x], axis=1), jnp.concatenate([x, other], axis=1))
+        g = g + got_g
+        s *= 2
+    return x, g
+
+
 def local(mass_bin, mobility_bin, intensity, basis_init, profile_init):
+    n_pix = lax.psum(1, "pix")
+    n_feat = lax.psum(1, "feat")
     rows = mass_bin.shape[0]
     block = math.gcd(rows, 32)
     count = rows // block
@@ -55,9 +96,11 @@
             precision=highest,
             preferred_element_type=jnp.float32,
         )
-        shared = lax.psum_scatter(partial_h, "feat", scatter_dimension=1, tiled=True)
-        numer_h = lax.psum(shared, "pix")
-        gram_w = lax.psum(partial_gram, ("pix", "feat"))
+        shared, gram_feat = halve_scatter(partial_h, partial_gram, "feat", n_feat)
+        both = double_sum(jnp.concatenate([shared, gram_feat], axis=1), "pix", n_pix)
+        width = shared.shape[1]
+        numer_h = both[:, :width]
+        gram_w = both[:, width:]
         profiles = (
             profiles
             * numer_h
@@ -66,12 +109,6 @@
                 + EPS
             )
         )
-        numer_w = lax.dot_general(
-            spectra,
-            lax.all_gather(profiles.astype(jnp.bfloat16), "feat", axis=1, tiled=True),
-            (((1,), (1,)), ((), ())),
-            preferred_element_type=jnp.float32,
-        )
         local_gram = lax.dot_general(
             profiles,
             profiles,
@@ -79,7 +116,13 @@
             precision=highest,
             preferred_element_type=jnp.float32,
         )
-        gram_h = lax.psum(local_gram, "feat")
+        profiles_all, gram_h = double_gather(profiles.astype(jnp.bfloat16), local_gram, "feat", n_feat)
+        numer_w = lax.dot_general(
+            spectra,
+            profiles_all,
+            (((1,), (1,)), ((), ())),
+            preferred_element_type=jnp.float32,
+        )
         basis = (
             basis
             * numer_w

time: 673 us -> 383 us (0.57)
  blocking collectives: 226 us -> 0 us
  waiting for transfers between devices: 200 us -> 114 us
  starting transfers between devices: 0.16 us -> 47.4 us
  between operations: 13.9 us -> 1.17 us
  matrix products: 146 us -> 139 us
    psum x4 -> x0, blocking collectives: 202 us -> none  [the longest x2 159 us: local(): gram_w = lax.psum(partial_gram, ('pix', 'feat'))]
    psum x2 -> x0, waiting for transfers between devices: 137 us -> none  [local(): numer_h = lax.psum(shared, 'pix')]
    ppermute x0 -> x28, waiting for transfers between devices: none -> 114 us  [the longest x10 48.2 us: double_sum(): x = x + lax.ppermute(x, axis, pairs(n, s))]
    reduce_scatter x2 -> x0, waiting for transfers between devices: 63.6 us -> none  [local(): lax.psum_scatter(partial_h, 'feat', scatter_dimension=1, tiled=True)]
    ppermute x0 -> x28, starting transfers between devices: none -> 47.4 us  [the longest x10 31.4 us: double_sum(): x = x + lax.ppermute(x, axis, pairs(n, s))]
    all_gather x2 -> x0, blocking collectives: 23.8 us -> none  [local(): lax.all_gather(profiles.astype(jnp.bfloat16), 'feat', axis=1, tiled=True)]
  transfers between devices with their start and end apart: 4 -> 28, of which waited for: 4 -> 26; matrix products, arithmetic and copies ran while one was open for 0% -> 0% of each run, Pallas kernels for 0% -> 0%
where the time goes in v1:
time: 383 us; the launch traced here: 379 us
  matrix products  139 us (36%)
  waiting for transfers between devices  114 us (30%)
  local copies, waits for them, and re-layouts  75.6 us (20%)
  starting transfers between devices  47.4 us (12%)
    dot_general x32, matrix products, bin_block(): jnp.einsum('pkb,pkm->pbm', mobility_hot, mass_hot, preferred_element_type...  117 us
    ppermute x10, waiting for transfers between devices, double_sum(): x = x + lax.ppermute(x, axis, pairs(n, s))  48.2 us
    ppermute x6, waiting for transfers between devices, halve_scatter(): got = lax.ppermute(jnp.concatenate([send, g], axis=1), axis, pairs(n, s))  43.9 us
    ppermute x10, starting transfers between devices, double_sum(): x = x + lax.ppermute(x, axis, pairs(n, s))  31.4 us
    eq x32, local copies, waits for them, and re-layouts, bin_block(): mass[:, :, None] == jnp.arange(MZ, dtype=jnp.int32)[None, None, :]  25 us
    dynamic_update_slice x32, local copies, waits for them, and re-layouts, local(): lax.map(bin_block, (mass_bin.reshape(count, block, PEAKS), mobility_bin.r...  23.3 us
    mul x32, local copies, waits for them, and re-layouts, bin_block(): (mass[:, :, None] == jnp.arange(MZ, dtype=jnp.int32)[None, None, :]).asty...  23 us
    ppermute x12, waiting for transfers between devices, double_gather(): other, got_g = lax.ppermute((x, g), axis, pairs(n, s))  21.7 us
  transfers between devices with their start and end apart: 28, of which 26 were waited for; matrix products, arithmetic and copies ran while one was open for 0% of the time, Pallas kernels for 0%

profile of v1, /device:TPU:16, one launch (start us, length us, event | category | flops | bytes accessed | tf_op | source)
XLA Modules:
  0.0 378.6 jit_solution(13462165123184856219)
XLA Ops:
  0.7 192.8 %while.10 = (s32[]{:T(128)}, bf16[32,32,4096]{2,1,0:T(8,128)(2,1)}, s32[32,32,256]{2,1,0:T(8,128)}, s32[32,32,256]{2,1,0:T(8,128)}, bf16[32,32,256]{2,1,0:T(8,128)(2,1)}, /*index=5*/s32[]{:T(128)}) while((s32[]{:T(128)}, bf16[32,32,4096]{2,1,0:T(8,128)(2,1)}, s32[32,32,256]{2,1,0:T(8,128)}, s32[32,32,256]{2,1,0:T(8,128)}, ...), condition=%wide.region_1.2_spmd, body=%wide.region_0.1_spmd.sunk | while | flops 71565312 | bytes 1557069 | solution.py:74
  2.2 3.7 fusion.65
  8.3 3.7 fusion.65
  14.3 3.7 fusion.65
  20.3 3.7 fusion.65
  26.3 3.7 fusion.65
  32.3 3.7 fusion.65
  38.4 3.7 fusion.65
  44.4 3.7 fusion.65
  50.4 3.7 fusion.65
  56.4 3.7 fusion.65
  62.5 3.7 fusion.65
  68.5 3.7 fusion.65
  74.5 3.7 fusion.65
  80.5 3.7 fusion.65
  86.5 3.7 fusion.65
  92.5 3.7 fusion.65
  98.6 3.7 fusion.65
  104.6 3.7 fusion.65
  110.7 3.7 fusion.65
  116.7 3.7 fusion.65
  122.7 3.7 fusion.65
  128.7 3.7 fusion.65
  134.7 3.7 fusion.65
  140.8 3.7 fusion.65
  146.8 3.7 fusion.65
  152.8 3.7 fusion.65
  158.9 3.7 fusion.65
  164.9 3.7 fusion.65
  170.9 3.7 fusion.65
  176.9 3.7 fusion.65
  183.0 3.7 fusion.65
  189.0 3.7 fusion.65
  193.9 4.9 %fusion.30 = f32[4096,64]{0,1:T(8,128)S(1)} fusion(bf16[1024,4096]{1,0:T(8,128)(2,1)} %bitcast.36, f32[1024,64]{0,1:T(8,128)S(1)} %copy-done), kind=kOutput, calls=%fused_computation.62 | convolution fusion | flops 536936448 | bytes 9699328 | tf_op jit(solution)/shard_map/dot_general | solution.py:86
  199.0 2.2 collective-permute-start
  201.1 13.8 %collective-permute-done = f32[64,2112]{1,0:T(8,128)S(1)} collective-permute-done((f32[64,2112]{1,0:T(8,128)S(1)}, f32[64,2112]{1,0:T(8,128)S(1)}, u32[]{:S(2)}, u32[]{:S(2)}) %collective-permute-start) | collective-permute-done | bytes 540704 | tf_op jit(solution)/shard_map/ppermute | solution.py:41
  216.4 6.6 %collective-permute-done.1 = f32[64,1088]{1,0:T(8,128)S(1)} collective-permute-done((f32[64,1088]{1,0:T(8,128)S(1)}, f32[64,1088]{1,0:T(8,128)S(1)}, u32[]{:S(2)}, u32[]{:S(2)}) %collective-permute-start.1) | collective-permute-done | bytes 278560 | tf_op jit(solution)/shard_map/ppermute | solution.py:41
  226.2 4.7 %collective-permute-done.3 = f32[64,576]{1,0:T(8,128)S(1)} collective-permute-done((f32[64,576]{1,0:T(8,128)S(1)}, f32[64,576]{1,0:T(8,128)S(1)}, u32[]{:S(2)}, u32[]{:S(2)}) %collective-permute-start.3) | collective-permute-done | bytes 147488 | tf_op jit(solution)/shard_map/ppermute | solution.py:51
  231.0 3.1 collective-permute-start.4
  234.1 3.9 %collective-permute-done.4 = f32[64,576]{1,0:T(8,128)S(1)} collective-permute-done((f32[64,576]{1,0:T(8,128)S(1)}, f32[64,576]{1,0:T(8,128)S(1)}, u32[]{:S(2)}, u32[]{:S(2)}) %collective-permute-start.4) | collective-permute-done | bytes 147488 | tf_op jit(solution)/shard_map/ppermute | solution.py:51
  238.1 2.0 collective-permute-start.5
  240.1 3.4 collective-permute-done.5
  243.5 3.4 collective-permute-start.6
  246.8 5.3 %collective-permute-done.6 = f32[64,576]{1,0:T(8,128)S(1)} collective-permute-done((f32[64,576]{1,0:T(8,128)S(1)}, f32[64,576]{1,0:T(8,128)S(1)}, u32[]{:S(2)}, u32[]{:S(2)}) %collective-permute-start.6) | collective-permute-done | bytes 147488 | tf_op jit(solution)/shard_map/ppermute | solution.py:51
  252.2 10.4 %collective-permute-start.7 = (f32[64,576]{1,0:T(8,128)S(1)}, f32[64,576]{1,0:T(8,128)S(1)}, u32[]{:S(2)}, u32[]{:S(2)}) collective-permute-start(f32[64,576]{1,0:T(8,128)S(1)} %add.166), channel_id=1, source_target_pairs={{0,128},{8,136},{16,144},{24,152},{32,160},{40,168},{48,176},{56,1... | collective-permute-start | bytes 442376 | tf_op jit(solution)/shard_map/ppermute | solution.py:51
  262.5 4.2 %collective-permute-done.7 = f32[64,576]{1,0:T(8,128)S(1)} collective-permute-done((f32[64,576]{1,0:T(8,128)S(1)}, f32[64,576]{1,0:T(8,128)S(1)}, u32[]{:S(2)}, u32[]{:S(2)}) %collective-permute-start.7) | collective-permute-done | bytes 147488 | tf_op jit(solution)/shard_map/ppermute | solution.py:51
  272.1 2.0 collective-permute-done.9
  275.3 2.8 collective-permute-start.13
  278.0 5.9 %collective-permute-done.13 = f32[64,64]{1,0:T(8,128)S(1)} collective-permute-done((f32[64,64]{1,0:T(8,128)S(1)}, f32[64,64]{1,0:T(8,128)S(1)}, u32[]{:S(2)}, u32[]{:S(2)}) %collective-permute-start.13) | collective-permute-done | bytes 16416 | tf_op jit(solution)/shard_map/ppermute | solution.py:60
  284.4 6.2 %fusion.13 = f32[1024,64]{0,1:T(8,128)S(1)} fusion(f32[1024,64]{0,1:T(8,128)S(1)} %fusion.11, f32[1024,64]{0,1:T(8,128)S(1)} %copy-done, bf16[1024,4096]{1,0:T(8,128)(2,1)} %bitcast.37, bf16[64,2048]{1,0:T(8,128)(2,1)S(1)} %maximum_select_fusion.4, bf16[64,2048]{1,0:T(8,128)(2,1)S(1)} %collective-permute-done.10, pred[]{:T(512)S(6)} %eq.55), kind=kOutput, calls=%fused_computation.20 | convolution fusion | flops 539361280 | bytes 9699329 | tf_op jit(solution)/shard_map/dot_general | solution.py:120
  290.6 5.1 %fusion.28 = f32[64,4096]{1,0:T(8,128)S(1)} fusion(bf16[1024,4096]{1,0:T(8,128)(2,1)} %bitcast.38, f32[1024,64]{0,1:T(8,128)S(1)} %fusion.13), kind=kOutput, calls=%fused_computation.60 | convolution fusion | flops 536936448 | bytes 9699328 | tf_op jit(solution)/shard_map/dot_general | solution.py:86
  296.6 14.5 %collective-permute-done.14 = f32[64,2112]{1,0:T(8,128)S(1)} collective-permute-done((f32[64,2112]{1,0:T(8,128)S(1)}, f32[64,2112]{1,0:T(8,128)S(1)}, u32[]{:S(2)}, u32[]{:S(2)}) %collective-permute-start.14) | collective-permute-done | bytes 540704 | tf_op jit(solution)/shard_map/ppermute | solution.py:41
  311.9 6.2 %collective-permute-done.15 = f32[64,1088]{1,0:T(8,128)S(1)} collective-permute-done((f32[64,1088]{1,0:T(8,128)S(1)}, f32[64,1088]{1,0:T(8,128)S(1)}, u32[]{:S(2)}, u32[]{:S(2)}) %collective-permute-start.15) | collective-permute-done | bytes 278560 | tf_op jit(solution)/shard_map/ppermute | solution.py:41
  321.3 4.8 %collective-permute-done.17 = f32[64,576]{1,0:T(8,128)S(1)} collective-permute-done((f32[64,576]{1,0:T(8,128)S(1)}, f32[64,576]{1,0:T(8,128)S(1)}, u32[]{:S(2)}, u32[]{:S(2)}) %collective-permute-start.17) | collective-permute-done | bytes 147488 | tf_op jit(solution)/shard_map/ppermute | solution.py:51
  326.1 3.1 collective-permute-start.18
  329.2 3.9 %collective-permute-done.18 = f32[64,576]{1,0:T(8,128)S(1)} collective-permute-done((f32[64,576]{1,0:T(8,128)S(1)}, f32[64,576]{1,0:T(8,128)S(1)}, u32[]{:S(2)}, u32[]{:S(2)}) %collective-permute-start.18) | collective-permute-done | bytes 147488 | tf_op jit(solution)/shard_map/ppermute | solution.py:51
  333.2 5.3 %collective-permute-done.19 = f32[64,576]{1,0:T(8,128)S(1)} collective-permute-done((f32[64,576]{1,0:T(8,128)S(1)}, f32[64,576]{1,0:T(8,128)S(1)}, u32[]{:S(2)}, u32[]{:S(2)}) %collective-permute-start.19) | collective-permute-done | bytes 147488 | tf_op jit(solution)/shard_map/ppermute | solution.py:51
  339.8 6.6 %collective-permute-done.20 = f32[64,576]{1,0:T(8,128)S(1)} collective-permute-done((f32[64,576]{1,0:T(8,128)S(1)}, f32[64,576]{1,0:T(8,128)S(1)}, u32[]{:S(2)}, u32[]{:S(2)}) %collective-permute-start.20) | collective-permute-done | bytes 147488 | tf_op jit(solution)/shard_map/ppermute | solution.py:51
  346.4 5.0 %collective-permute-start.21 = (f32[64,576]{1,0:T(8,128)S(1)}, f32[64,576]{1,0:T(8,128)S(1)}, u32[]{:S(2)}, u32[]{:S(2)}) collective-permute-start(f32[64,576]{1,0:T(8,128)S(1)} %add.183), channel_id=1, source_target_pairs={{0,128},{8,136},{16,144},{24,152},{32,160},{40,168},{48,176},{56,1... | collective-permute-start | bytes 442376 | tf_op jit(solution)/shard_map/ppermute | solution.py:51
  351.4 6.1 %collective-permute-done.21 = f32[64,576]{1,0:T(8,128)S(1)} collective-permute-done((f32[64,576]{1,0:T(8,128)S(1)}, f32[64,576]{1,0:T(8,128)S(1)}, u32[]{:S(2)}, u32[]{:S(2)}) %collective-permute-start.21) | collective-permute-done | bytes 147488 | tf_op jit(solution)/shard_map/ppermute | solution.py:51
  362.9 2.3 collective-permute-done.23
  365.5 3.4 collective-permute-start.27
  369.0 5.8 %collective-permute-done.27 = f32[64,64]{1,0:T(8,128)S(1)} collective-permute-done((f32[64,64]{1,0:T(8,128)S(1)}, f32[64,64]{1,0:T(8,128)S(1)}, u32[]{:S(2)}, u32[]{:S(2)}) %collective-permute-start.27) | collective-permute-done | bytes 16416 | tf_op jit(solution)/shard_map/ppermute | solution.py:60
  375.2 3.4 fusion.12
  (221 shorter events, 99.8 us)
Async XLA Ops:
  0.7 192.9 %copy-start = (f32[1024,64]{0,1:T(8,128)S(1)}, f32[1024,64]{0,1:T(8,128)}, u32[]{:S(2)}) copy-start(f32[1024,64]{0,1:T(8,128)} %param.10) | copy-start | bytes 786436
  198.9 67.9 %copy-start.2 = (f32[64,512]{1,0:T(8,128)S(1)}, f32[64,512]{1,0:T(8,128)}, u32[]{:S(2)}) copy-start(f32[64,512]{1,0:T(8,128)} %param.11) | copy-start | bytes 393220
  199.0 16.0 %collective-permute-start = (f32[64,2112]{1,0:T(8,128)S(1)}, f32[64,2112]{1,0:T(8,128)S(1)}, u32[]{:S(2)}, u32[]{:S(2)}) collective-permute-start(f32[64,2112]{1,0:T(8,128)S(1)} %pad_maximum_fusion), channel_id=1, source_target_pairs={{0,4},{1,5},{2,6},{3,7},{4,0},{5,1},{6,2},{7,3},{8,12},{9,13},{10,... | collective-permute-start | bytes 1622024 | tf_op jit(solution)/shard_map/ppermute | solution.py:41
  215.1 8.0 %collective-permute-start.1 = (f32[64,1088]{1,0:T(8,128)S(1)}, f32[64,1088]{1,0:T(8,128)S(1)}, u32[]{:S(2)}, u32[]{:S(2)}) collective-permute-start(f32[64,1088]{1,0:T(8,128)S(1)} %pad_maximum_fusion.2), channel_id=1, source_target_pairs={{0,2},{1,3},{2,0},{3,1},{4,6},{5,7},{6,4},{7,5},{8,10},{9,11},{10,... | collective-permute-start | bytes 835592 | tf_op jit(solution)/shard_map/ppermute | solution.py:41
  223.1 1.5 collective-permute-start.2
  224.7 6.3 %collective-permute-start.3 = (f32[64,576]{1,0:T(8,128)S(1)}, f32[64,576]{1,0:T(8,128)S(1)}, u32[]{:S(2)}, u32[]{:S(2)}) collective-permute-start(f32[64,576]{1,0:T(8,128)S(1)} %pad_maximum_fusion.5), channel_id=1, source_target_pairs={{0,8},{8,0},{16,24},{24,16},{32,40},{40,32},{48,56},{56,48},{64,72... | collective-permute-start | bytes 442376 | tf_op jit(solution)/shard_map/ppermute | solution.py:51
  231.0 7.0 %collective-permute-start.4 = (f32[64,576]{1,0:T(8,128)S(1)}, f32[64,576]{1,0:T(8,128)S(1)}, u32[]{:S(2)}, u32[]{:S(2)}) collective-permute-start(f32[64,576]{1,0:T(8,128)S(1)} %fusion.39), channel_id=1, source_target_pairs={{0,16},{8,24},{16,0},{24,8},{32,48},{40,56},{48,32},{56,40},{64,80... | collective-permute-start | bytes 442376 | tf_op jit(solution)/shard_map/ppermute | solution.py:51
  238.1 5.4 %collective-permute-start.5 = (f32[64,576]{1,0:T(8,128)S(1)}, f32[64,576]{1,0:T(8,128)S(1)}, u32[]{:S(2)}, u32[]{:S(2)}) collective-permute-start(f32[64,576]{1,0:T(8,128)S(1)} %add.164), channel_id=1, source_target_pairs={{0,32},{8,40},{16,48},{24,56},{32,0},{40,8},{48,16},{56,24},{64,96... | collective-permute-start | bytes 442376 | tf_op jit(solution)/shard_map/ppermute | solution.py:51
  243.5 8.7 %collective-permute-start.6 = (f32[64,576]{1,0:T(8,128)S(1)}, f32[64,576]{1,0:T(8,128)S(1)}, u32[]{:S(2)}, u32[]{:S(2)}) collective-permute-start(f32[64,576]{1,0:T(8,128)S(1)} %add.165), channel_id=1, source_target_pairs={{0,64},{8,72},{16,80},{24,88},{32,96},{40,104},{48,112},{56,120},{... | collective-permute-start | bytes 442376 | tf_op jit(solution)/shard_map/ppermute | solution.py:51
  252.2 14.6 %collective-permute-start.7 = (f32[64,576]{1,0:T(8,128)S(1)}, f32[64,576]{1,0:T(8,128)S(1)}, u32[]{:S(2)}, u32[]{:S(2)}) collective-permute-start(f32[64,576]{1,0:T(8,128)S(1)} %add.166), channel_id=1, source_target_pairs={{0,128},{8,136},{16,144},{24,152},{32,160},{40,168},{48,176},{56,1... | collective-permute-start | bytes 442376 | tf_op jit(solution)/shard_map/ppermute | solution.py:51
  267.0 1.3 collective-permute-start.8
  268.4 5.6 %collective-permute-start.9 = (bf16[64,1024]{1,0:T(8,128)(2,1)S(1)}, bf16[64,1024]{1,0:T(8,128)(2,1)S(1)}, u32[]{:S(2)}, u32[]{:S(2)}) collective-permute-start(bf16[64,1024]{1,0:T(8,128)(2,1)S(1)} %maximum_select_fusion.6), channel_id=1, source_target_pairs={{0,2},{1,3},{2,0},{3,1},{4,6},{5,7},{6,4},{7,5},{8,10},{9,11},{10,... | collective-permute-start | bytes 393224 | tf_op jit(solution)/shard_map/ppermute | solution.py:60
  270.0 1.3 collective-permute-start.11
  271.3 3.9 %collective-permute-start.12 = (f32[64,64]{1,0:T(8,128)S(1)}, f32[64,64]{1,0:T(8,128)S(1)}, u32[]{:S(2)}, u32[]{:S(2)}) collective-permute-start(f32[64,64]{1,0:T(8,128)S(1)} %add.169), channel_id=1, source_target_pairs={{0,2},{1,3},{2,0},{3,1},{4,6},{5,7},{6,4},{7,5},{8,10},{9,11},{10,... | collective-permute-start | bytes 49160 | tf_op jit(solution)/shard_map/ppermute | solution.py:60
  274.1 10.3 %collective-permute-start.10 = (bf16[64,2048]{1,0:T(8,128)(2,1)S(1)}, bf16[64,2048]{1,0:T(8,128)(2,1)S(1)}, u32[]{:S(2)}, u32[]{:S(2)}) collective-permute-start(bf16[64,2048]{1,0:T(8,128)(2,1)S(1)} %maximum_select_fusion.4), channel_id=1, source_target_pairs={{0,4},{1,5},{2,6},{3,7},{4,0},{5,1},{6,2},{7,3},{8,12},{9,13},{10,... | collective-permute-start | bytes 786440 | tf_op jit(solution)/shard_map/ppermute | solution.py:60
  275.3 8.7 %collective-permute-start.13 = (f32[64,64]{1,0:T(8,128)S(1)}, f32[64,64]{1,0:T(8,128)S(1)}, u32[]{:S(2)}, u32[]{:S(2)}) collective-permute-start(f32[64,64]{1,0:T(8,128)S(1)} %add.170), channel_id=1, source_target_pairs={{0,4},{1,5},{2,6},{3,7},{4,0},{5,1},{6,2},{7,3},{8,12},{9,13},{10,... | collective-permute-start | bytes 49160 | tf_op jit(solution)/shard_map/ppermute | solution.py:60
  284.4 90.8 %slice-start = ((s8[8388608]{0:T(1024)(128)(4,1)}), s8[4194304]{0:T(1024)(128)(4,1)S(1)}, s32[]{:S(2)}) async-start(s8[8388608]{0:T(1024)(128)(4,1)} %bitcast.39), calls=%async_computation | async-start | bytes 8388608
  290.6 84.6 %slice-start.1 = ((s8[8388608]{0:T(1024)(128)(4,1)}), s8[4194304]{0:T(1024)(128)(4,1)S(1)}, s32[]{:S(2)}) async-start(s8[8388608]{0:T(1024)(128)(4,1)} %bitcast.39), calls=%async_computation.1 | async-start | bytes 8388608
  296.2 15.0 %collective-permute-start.14 = (f32[64,2112]{1,0:T(8,128)S(1)}, f32[64,2112]{1,0:T(8,128)S(1)}, u32[]{:S(2)}, u32[]{:S(2)}) collective-permute-start(f32[64,2112]{1,0:T(8,128)S(1)} %pad_maximum_fusion.1), channel_id=1, source_target_pairs={{0,4},{1,5},{2,6},{3,7},{4,0},{5,1},{6,2},{7,3},{8,12},{9,13},{10,... | collective-permute-start | bytes 1622024 | tf_op jit(solution)/shard_map/ppermute | solution.py:41
  311.3 6.8 %collective-permute-start.15 = (f32[64,1088]{1,0:T(8,128)S(1)}, f32[64,1088]{1,0:T(8,128)S(1)}, u32[]{:S(2)}, u32[]{:S(2)}) collective-permute-start(f32[64,1088]{1,0:T(8,128)S(1)} %pad_maximum_fusion.3), channel_id=1, source_target_pairs={{0,2},{1,3},{2,0},{3,1},{4,6},{5,7},{6,4},{7,5},{8,10},{9,11},{10,... | collective-permute-start | bytes 835592 | tf_op jit(solution)/shard_map/ppermute | solution.py:41
  318.2 1.5 collective-permute-start.16
  319.8 6.3 %collective-permute-start.17 = (f32[64,576]{1,0:T(8,128)S(1)}, f32[64,576]{1,0:T(8,128)S(1)}, u32[]{:S(2)}, u32[]{:S(2)}) collective-permute-start(f32[64,576]{1,0:T(8,128)S(1)} %pad_maximum_fusion.7), channel_id=1, source_target_pairs={{0,8},{8,0},{16,24},{24,16},{32,40},{40,32},{48,56},{56,48},{64,72... | collective-permute-start | bytes 442376 | tf_op jit(solution)/shard_map/ppermute | solution.py:51
  326.1 7.0 %collective-permute-start.18 = (f32[64,576]{1,0:T(8,128)S(1)}, f32[64,576]{1,0:T(8,128)S(1)}, u32[]{:S(2)}, u32[]{:S(2)}) collective-permute-start(f32[64,576]{1,0:T(8,128)S(1)} %fusion.38), channel_id=1, source_target_pairs={{0,16},{8,24},{16,0},{24,8},{32,48},{40,56},{48,32},{56,40},{64,80... | collective-permute-start | bytes 442376 | tf_op jit(solution)/shard_map/ppermute | solution.py:51
  333.1 5.4 %collective-permute-start.19 = (f32[64,576]{1,0:T(8,128)S(1)}, f32[64,576]{1,0:T(8,128)S(1)}, u32[]{:S(2)}, u32[]{:S(2)}) collective-permute-start(f32[64,576]{1,0:T(8,128)S(1)} %add.181), channel_id=1, source_target_pairs={{0,32},{8,40},{16,48},{24,56},{32,0},{40,8},{48,16},{56,24},{64,96... | collective-permute-start | bytes 442376 | tf_op jit(solution)/shard_map/ppermute | solution.py:51
  338.6 7.8 %collective-permute-start.20 = (f32[64,576]{1,0:T(8,128)S(1)}, f32[64,576]{1,0:T(8,128)S(1)}, u32[]{:S(2)}, u32[]{:S(2)}) collective-permute-start(f32[64,576]{1,0:T(8,128)S(1)} %add.182), channel_id=1, source_target_pairs={{0,64},{8,72},{16,80},{24,88},{32,96},{40,104},{48,112},{56,120},{... | collective-permute-start | bytes 442376 | tf_op jit(solution)/shard_map/ppermute | solution.py:51
  346.4 11.1 %collective-permute-start.21 = (f32[64,576]{1,0:T(8,128)S(1)}, f32[64,576]{1,0:T(8,128)S(1)}, u32[]{:S(2)}, u32[]{:S(2)}) collective-permute-start(f32[64,576]{1,0:T(8,128)S(1)} %add.183), channel_id=1, source_target_pairs={{0,128},{8,136},{16,144},{24,152},{32,160},{40,168},{48,176},{56,1... | collective-permute-start | bytes 442376 | tf_op jit(solution)/shard_map/ppermute | solution.py:51
  357.8 20.8 %copy-start.1 = (f32[64,512]{1,0:T(8,128)}, f32[64,512]{1,0:T(8,128)S(1)}, u32[]{:S(2)}) copy-start(f32[64,512]{1,0:T(8,128)S(1)} %get-tuple-element.45) | copy-start | bytes 393220
  357.8 1.3 collective-permute-start.22
  359.2 6.0 %collective-permute-start.23 = (bf16[64,1024]{1,0:T(8,128)(2,1)S(1)}, bf16[64,1024]{1,0:T(8,128)(2,1)S(1)}, u32[]{:S(2)}, u32[]{:S(2)}) collective-permute-start(bf16[64,1024]{1,0:T(8,128)(2,1)S(1)} %maximum_select_fusion.7), channel_id=1, source_target_pairs={{0,2},{1,3},{2,0},{3,1},{4,6},{5,7},{6,4},{7,5},{8,10},{9,11},{10,... | collective-permute-start | bytes 393224 | tf_op jit(solution)/shard_map/ppermute | solution.py:60
  360.0 1.3 collective-permute-start.25
  361.3 4.2 %collective-permute-start.26 = (f32[64,64]{1,0:T(8,128)S(1)}, f32[64,64]{1,0:T(8,128)S(1)}, u32[]{:S(2)}, u32[]{:S(2)}) collective-permute-start(f32[64,64]{1,0:T(8,128)S(1)} %add.186), channel_id=1, source_target_pairs={{0,2},{1,3},{2,0},{3,1},{4,6},{5,7},{6,4},{7,5},{8,10},{9,11},{10,... | collective-permute-start | bytes 49160 | tf_op jit(solution)/shard_map/ppermute | solution.py:60
  365.3 9.9 %collective-permute-start.24 = (bf16[64,2048]{1,0:T(8,128)(2,1)S(1)}, bf16[64,2048]{1,0:T(8,128)(2,1)S(1)}, u32[]{:S(2)}, u32[]{:S(2)}) collective-permute-start(bf16[64,2048]{1,0:T(8,128)(2,1)S(1)} %maximum_select_fusion.5), channel_id=1, source_target_pairs={{0,4},{1,5},{2,6},{3,7},{4,0},{5,1},{6,2},{7,3},{8,12},{9,13},{10,... | collective-permute-start | bytes 786440 | tf_op jit(solution)/shard_map/ppermute | solution.py:60
  365.5 9.2 %collective-permute-start.27 = (f32[64,64]{1,0:T(8,128)S(1)}, f32[64,64]{1,0:T(8,128)S(1)}, u32[]{:S(2)}, u32[]{:S(2)}) collective-permute-start(f32[64,64]{1,0:T(8,128)S(1)} %add.187), channel_id=1, source_target_pairs={{0,4},{1,5},{2,6},{3,7},{4,0},{5,1},{6,2},{7,3},{8,12},{9,13},{10,... | collective-permute-start | bytes 49160 | tf_op jit(solution)/shard_map/ppermute | solution.py:60

commit v2 on v1

--- a/solution.py
+++ b/solution.py
@@ -9,6 +9,7 @@
 MOB = 16
 PEAKS = 256
 ITERS = 2
+SIDE = 64
 
 
 EPS = 1e-06
@@ -16,13 +17,13 @@
 
 def bin_block(args):
     mass, mobility, weight = args
-    mass_hot = (mass[:, :, None] == jnp.arange(MZ, dtype=jnp.int32)[None, None, :]).astype(
-        jnp.bfloat16
-    ) * weight[:, :, None]
-    mobility_hot = (mobility[:, :, None] == jnp.arange(MOB, dtype=jnp.int32)[None, None, :]).astype(
-        jnp.bfloat16
-    )
-    dense = jnp.einsum("pkb,pkm->pbm", mobility_hot, mass_hot, preferred_element_type=jnp.float32)
+    feature = mobility * MZ + mass
+    hi = feature // SIDE
+    lo = feature % SIDE
+    side = jnp.arange(SIDE, dtype=jnp.int32)
+    hi_hot = (hi[:, :, None] == side[None, None, :]).astype(jnp.bfloat16) * weight[:, :, None]
+    lo_hot = (lo[:, :, None] == side[None, None, :]).astype(jnp.bfloat16)
+    dense = jnp.einsum("pkh,pkl->phl", hi_hot, lo_hot, preferred_element_type=jnp.float32)
     return dense.reshape(mass.shape[0], MZ * MOB).astype(jnp.bfloat16)
 
 
@@ -69,7 +70,7 @@
     n_pix = lax.psum(1, "pix")
     n_feat = lax.psum(1, "feat")
     rows = mass_bin.shape[0]
-    block = math.gcd(rows, 32)
+    block = math.gcd(rows, 1024)
     count = rows // block
     spectra = lax.map(
         bin_block,

time: 383 us -> 229 us (0.60)
  matrix products: 139 us -> 43.3 us
  local copies, waits for them, and re-layouts: 75.6 us -> 18.6 us
    dot_general x32 -> x1, matrix products: 117 us -> 21.1 us  [bin_block(): jnp.einsum('pkh,pkl->phl', hi_hot, lo_hot, preferred_element_type=jnp.flo...]
    eq x32 -> x0, local copies, waits for them, and re-layouts: 25 us -> none  [bin_block(): mass[:, :, None] == jnp.arange(MZ, dtype=jnp.int32)[None, None, :]]
    dynamic_update_slice x32 -> x0, local copies, waits for them, and re-layouts: 23.3 us -> none  [local(): lax.map(bin_block, (mass_bin.reshape(count, block, PEAKS), mobility_bin.r...]
    mul x32 -> x0, local copies, waits for them, and re-layouts: 23 us -> none  [bin_block(): (mass[:, :, None] == jnp.arange(MZ, dtype=jnp.int32)[None, None, :]).asty...]
    convert_element_type x32 -> x1, local copies, waits for them, and re-layouts: 4.13 us -> 18.4 us  [bin_block(): return dense.reshape(mass.shape[0], MZ * MOB).astype(jnp.bfloat16)]
  transfers between devices with their start and end apart: 28 -> 28, of which waited for: 26 -> 26; matrix products, arithmetic and copies ran while one was open for 0% -> 1% of each run, Pallas kernels for 0% -> 0%
where the time goes in v2:
time: 229 us; the launch traced here: 228 us
  waiting for transfers between devices  114 us (50%)
  starting transfers between devices  47.7 us (21%)
  matrix products  43.3 us (19%)
  local copies, waits for them, and re-layouts  18.6 us (8%)
  other arithmetic  3.34 us (1%)
    ppermute x10, waiting for transfers between devices, double_sum(): x = x + lax.ppermute(x, axis, pairs(n, s))  48.1 us
    ppermute x6, waiting for transfers between devices, halve_scatter(): got = lax.ppermute(jnp.concatenate([send, g], axis=1), axis, pairs(n, s))  43.9 us
    ppermute x10, starting transfers between devices, double_sum(): x = x + lax.ppermute(x, axis, pairs(n, s))  31.9 us
    ppermute x12, waiting for transfers between devices, double_gather(): other, got_g = lax.ppermute((x, g), axis, pairs(n, s))  21.9 us
    dot_general x1, matrix products, bin_block(): jnp.einsum('pkh,pkl->phl', hi_hot, lo_hot, preferred_element_type=jnp.flo...  21.1 us
    convert_element_type x1, local copies, waits for them, and re-layouts, bin_block(): return dense.reshape(mass.shape[0], MZ * MOB).astype(jnp.bfloat16)  18.4 us
    dot_general x2, matrix products, local(): lax.dot_general(basis.astype(jnp.bfloat16), spectra, (((0,), (0,)), ((),...  12.2 us
    ppermute x12, starting transfers between devices, double_gather(): other, got_g = lax.ppermute((x, g), axis, pairs(n, s))  11.1 us
  transfers between devices with their start and end apart: 28, of which 26 were waited for; matrix products, arithmetic and copies ran while one was open for 1% of the time, Pallas kernels for 0%

profile of v2, /device:TPU:16, one launch (start us, length us, event | category | flops | bytes accessed | tf_op | source)
XLA Modules:
  0.0 228.1 jit_solution(1350269733385332116)
XLA Ops:
  0.7 2.5 %add_select_fusion.1 = (s32[1024,256]{1,0:T(8,128)S(1)}, s32[1024,256]{1,0:T(8,128)S(1)}) fusion(s32[1024,256]{1,0:T(8,128)} %param.5, s32[1024,256]{1,0:T(8,128)} %param.6), kind=kLoop, calls=%fused_computation.10 | loop fusion | flops 5505024 | bytes 4194304 | tf_op jit(solution)/shard_map/while/body/eval_jaxpr/jit(floor_divide)/jit(_where)/select_n | solution.py:21
  3.2 21.1 %fusion.7 = bf16[1024,64,64]{2,1,0:T(8,128)(2,1)} fusion(s32[1024,256]{1,0:T(8,128)S(1)} %get-tuple-element.13, s32[1024,256]{1,0:T(8,128)S(1)} %get-tuple-element.12, bf16[1024,256]{1,0:T(8,128)(2,1)} %param.7), kind=kOutput, calls=%fused_computation.8 | convolution fusion | flops 2202009600 | bytes 11010048 | tf_op jit(solution)/shard_map/while/body/eval_jaxpr/pkh,pkl->phl/dot_general | solution.py:26
  24.2 18.4 %copy.7 = bf16[1024,64,64]{0,2,1:T(8,128)(2,1)} copy(bf16[1024,64,64]{2,1,0:T(8,128)(2,1)} %fusion.7) | data formatting | bytes 16777216 | tf_op jit(solution)/shard_map/while/body/eval_jaxpr/convert_element_type | solution.py:27
  42.7 0.4 fusion.44
  43.0 6.0 %fusion.31 = f32[4096,64]{0,1:T(8,128)S(1)} fusion(bf16[1024,4096]{0,1:T(8,128)(2,1)} %bitcast.23, f32[1024,64]{0,1:T(8,128)S(1)} %copy-done), kind=kOutput, calls=%fused_computation.66 | convolution fusion | flops 536936448 | bytes 9699328 | tf_op jit(solution)/shard_map/dot_general | solution.py:87
  49.2 2.1 collective-permute-start
  51.3 13.8 %collective-permute-done = f32[64,2112]{1,0:T(8,128)S(1)} collective-permute-done((f32[64,2112]{1,0:T(8,128)S(1)}, f32[64,2112]{1,0:T(8,128)S(1)}, u32[]{:S(2)}, u32[]{:S(2)}) %collective-permute-start) | collective-permute-done | bytes 540704 | tf_op jit(solution)/shard_map/ppermute | solution.py:42
  65.2 1.4 collective-permute-start.1
  66.6 6.6 %collective-permute-done.1 = f32[64,1088]{1,0:T(8,128)S(1)} collective-permute-done((f32[64,1088]{1,0:T(8,128)S(1)}, f32[64,1088]{1,0:T(8,128)S(1)}, u32[]{:S(2)}, u32[]{:S(2)}) %collective-permute-start.1) | collective-permute-done | bytes 278560 | tf_op jit(solution)/shard_map/ppermute | solution.py:42
  73.4 1.4 collective-permute-done.2
  74.8 1.6 collective-permute-start.3
  76.4 4.7 %collective-permute-done.3 = f32[64,576]{1,0:T(8,128)S(1)} collective-permute-done((f32[64,576]{1,0:T(8,128)S(1)}, f32[64,576]{1,0:T(8,128)S(1)}, u32[]{:S(2)}, u32[]{:S(2)}) %collective-permute-start.3) | collective-permute-done | bytes 147488 | tf_op jit(solution)/shard_map/ppermute | solution.py:52
  81.2 3.1 %collective-permute-start.4 = (f32[64,576]{1,0:T(8,128)S(1)}, f32[64,576]{1,0:T(8,128)S(1)}, u32[]{:S(2)}, u32[]{:S(2)}) collective-permute-start(f32[64,576]{1,0:T(8,128)S(1)} %fusion.41), channel_id=1, source_target_pairs={{0,16},{8,24},{16,0},{24,8},{32,48},{40,56},{48,32},{56,40},{64,80... | collective-permute-start | bytes 442376 | tf_op jit(solution)/shard_map/ppermute | solution.py:52
  84.3 3.9 %collective-permute-done.4 = f32[64,576]{1,0:T(8,128)S(1)} collective-permute-done((f32[64,576]{1,0:T(8,128)S(1)}, f32[64,576]{1,0:T(8,128)S(1)}, u32[]{:S(2)}, u32[]{:S(2)}) %collective-permute-start.4) | collective-permute-done | bytes 147488 | tf_op jit(solution)/shard_map/ppermute | solution.py:52
  88.2 2.2 collective-permute-start.5
  90.4 3.4 %collective-permute-done.5 = f32[64,576]{1,0:T(8,128)S(1)} collective-permute-done((f32[64,576]{1,0:T(8,128)S(1)}, f32[64,576]{1,0:T(8,128)S(1)}, u32[]{:S(2)}, u32[]{:S(2)}) %collective-permute-start.5) | collective-permute-done | bytes 147488 | tf_op jit(solution)/shard_map/ppermute | solution.py:52
  93.8 3.4 %collective-permute-start.6 = (f32[64,576]{1,0:T(8,128)S(1)}, f32[64,576]{1,0:T(8,128)S(1)}, u32[]{:S(2)}, u32[]{:S(2)}) collective-permute-start(f32[64,576]{1,0:T(8,128)S(1)} %add.185), channel_id=1, source_target_pairs={{0,64},{8,72},{16,80},{24,88},{32,96},{40,104},{48,112},{56,120},{... | collective-permute-start | bytes 442376 | tf_op jit(solution)/shard_map/ppermute | solution.py:52
  97.2 5.3 %collective-permute-done.6 = f32[64,576]{1,0:T(8,128)S(1)} collective-permute-done((f32[64,576]{1,0:T(8,128)S(1)}, f32[64,576]{1,0:T(8,128)S(1)}, u32[]{:S(2)}, u32[]{:S(2)}) %collective-permute-start.6) | collective-permute-done | bytes 147488 | tf_op jit(solution)/shard_map/ppermute | solution.py:52
  102.5 10.4 %collective-permute-start.7 = (f32[64,576]{1,0:T(8,128)S(1)}, f32[64,576]{1,0:T(8,128)S(1)}, u32[]{:S(2)}, u32[]{:S(2)}) collective-permute-start(f32[64,576]{1,0:T(8,128)S(1)} %add.186), channel_id=1, source_target_pairs={{0,128},{8,136},{16,144},{24,152},{32,160},{40,168},{48,176},{56,1... | collective-permute-start | bytes 442376 | tf_op jit(solution)/shard_map/ppermute | solution.py:52
  112.9 4.2 %collective-permute-done.7 = f32[64,576]{1,0:T(8,128)S(1)} collective-permute-done((f32[64,576]{1,0:T(8,128)S(1)}, f32[64,576]{1,0:T(8,128)S(1)}, u32[]{:S(2)}, u32[]{:S(2)}) %collective-permute-start.7) | collective-permute-done | bytes 147488 | tf_op jit(solution)/shard_map/ppermute | solution.py:52
  117.1 0.3 fusion.42
  117.5 1.2 collective-permute-done.8
  118.8 1.4 collective-permute-start.9
  120.1 0.3 fusion.45
  120.5 1.2 collective-permute-done.11
  121.7 0.7 collective-permute-start.12
  122.4 2.0 collective-permute-done.9
  124.5 0.4 collective-permute-start.10
  124.9 0.7 collective-permute-done.12
  125.6 2.6 %collective-permute-start.13 = (f32[64,64]{1,0:T(8,128)S(1)}, f32[64,64]{1,0:T(8,128)S(1)}, u32[]{:S(2)}, u32[]{:S(2)}) collective-permute-start(f32[64,64]{1,0:T(8,128)S(1)} %add.190), channel_id=1, source_target_pairs={{0,4},{1,5},{2,6},{3,7},{4,0},{5,1},{6,2},{7,3},{8,12},{9,13},{10,... | collective-permute-start | bytes 49160 | tf_op jit(solution)/shard_map/ppermute | solution.py:61
  128.2 6.1 %collective-permute-done.13 = f32[64,64]{1,0:T(8,128)S(1)} collective-permute-done((f32[64,64]{1,0:T(8,128)S(1)}, f32[64,64]{1,0:T(8,128)S(1)}, u32[]{:S(2)}, u32[]{:S(2)}) %collective-permute-start.13) | collective-permute-done | bytes 16416 | tf_op jit(solution)/shard_map/ppermute | solution.py:61
  134.3 0.4 fusion.10
  134.8 5.1 %fusion.12 = f32[1024,64]{0,1:T(8,128)S(1)} fusion(f32[1024,64]{0,1:T(8,128)S(1)} %fusion.10, f32[1024,64]{0,1:T(8,128)S(1)} %copy-done, bf16[1024,4096]{0,1:T(8,128)(2,1)} %bitcast.24, bf16[64,2048]{1,0:T(8,128)(2,1)S(1)} %maximum_select_fusion.4, bf16[64,2048]{1,0:T(8,128)(2,1)S(1)} %collective-permute-done.10, pred[]{:T(512)S(6)} %eq.71), kind=kOutput, calls=%fused_computation.20 | convolution fusion | flops 539361280 | bytes 9699329 | tf_op jit(solution)/shard_map/dot_general | solution.py:121
  139.9 6.2 %fusion.29 = f32[64,4096]{1,0:T(8,128)S(1)} fusion(bf16[1024,4096]{0,1:T(8,128)(2,1)} %bitcast.25, f32[1024,64]{0,1:T(8,128)S(1)} %fusion.12), kind=kOutput, calls=%fused_computation.64 | convolution fusion | flops 536936448 | bytes 9699328 | tf_op jit(solution)/shard_map/dot_general | solution.py:87
  146.1 0.4 fusion.46
  146.6 0.4 collective-permute-start.14
  147.0 14.6 %collective-permute-done.14 = f32[64,2112]{1,0:T(8,128)S(1)} collective-permute-done((f32[64,2112]{1,0:T(8,128)S(1)}, f32[64,2112]{1,0:T(8,128)S(1)}, u32[]{:S(2)}, u32[]{:S(2)}) %collective-permute-start.14) | collective-permute-done | bytes 540704 | tf_op jit(solution)/shard_map/ppermute | solution.py:42
  161.7 0.6 collective-permute-start.15
  162.2 6.2 %collective-permute-done.15 = f32[64,1088]{1,0:T(8,128)S(1)} collective-permute-done((f32[64,1088]{1,0:T(8,128)S(1)}, f32[64,1088]{1,0:T(8,128)S(1)}, u32[]{:S(2)}, u32[]{:S(2)}) %collective-permute-start.15) | collective-permute-done | bytes 278560 | tf_op jit(solution)/shard_map/ppermute | solution.py:42
  168.6 0.1 collective-permute-start.16
  168.7 1.4 collective-permute-done.16
  170.1 1.6 collective-permute-start.17
  171.7 4.8 %collective-permute-done.17 = f32[64,576]{1,0:T(8,128)S(1)} collective-permute-done((f32[64,576]{1,0:T(8,128)S(1)}, f32[64,576]{1,0:T(8,128)S(1)}, u32[]{:S(2)}, u32[]{:S(2)}) %collective-permute-start.17) | collective-permute-done | bytes 147488 | tf_op jit(solution)/shard_map/ppermute | solution.py:52
  176.5 3.3 %collective-permute-start.18 = (f32[64,576]{1,0:T(8,128)S(1)}, f32[64,576]{1,0:T(8,128)S(1)}, u32[]{:S(2)}, u32[]{:S(2)}) collective-permute-start(f32[64,576]{1,0:T(8,128)S(1)} %fusion.40), channel_id=1, source_target_pairs={{0,16},{8,24},{16,0},{24,8},{32,48},{40,56},{48,32},{56,40},{64,80... | collective-permute-start | bytes 442376 | tf_op jit(solution)/shard_map/ppermute | solution.py:52
  179.8 3.9 %collective-permute-done.18 = f32[64,576]{1,0:T(8,128)S(1)} collective-permute-done((f32[64,576]{1,0:T(8,128)S(1)}, f32[64,576]{1,0:T(8,128)S(1)}, u32[]{:S(2)}, u32[]{:S(2)}) %collective-permute-start.18) | collective-permute-done | bytes 147488 | tf_op jit(solution)/shard_map/ppermute | solution.py:52
  183.7 0.1 collective-permute-start.19
  183.8 5.3 %collective-permute-done.19 = f32[64,576]{1,0:T(8,128)S(1)} collective-permute-done((f32[64,576]{1,0:T(8,128)S(1)}, f32[64,576]{1,0:T(8,128)S(1)}, u32[]{:S(2)}, u32[]{:S(2)}) %collective-permute-start.19) | collective-permute-done | bytes 147488 | tf_op jit(solution)/shard_map/ppermute | solution.py:52
  189.2 1.3 collective-permute-start.20
  190.4 6.6 %collective-permute-done.20 = f32[64,576]{1,0:T(8,128)S(1)} collective-permute-done((f32[64,576]{1,0:T(8,128)S(1)}, f32[64,576]{1,0:T(8,128)S(1)}, u32[]{:S(2)}, u32[]{:S(2)}) %collective-permute-start.20) | collective-permute-done | bytes 147488 | tf_op jit(solution)/shard_map/ppermute | solution.py:52
  197.0 5.0 %collective-permute-start.21 = (f32[64,576]{1,0:T(8,128)S(1)}, f32[64,576]{1,0:T(8,128)S(1)}, u32[]{:S(2)}, u32[]{:S(2)}) collective-permute-start(f32[64,576]{1,0:T(8,128)S(1)} %add.203), channel_id=1, source_target_pairs={{0,128},{8,136},{16,144},{24,152},{32,160},{40,168},{48,176},{56,1... | collective-permute-start | bytes 442376 | tf_op jit(solution)/shard_map/ppermute | solution.py:52
  202.0 6.1 %collective-permute-done.21 = f32[64,576]{1,0:T(8,128)S(1)} collective-permute-done((f32[64,576]{1,0:T(8,128)S(1)}, f32[64,576]{1,0:T(8,128)S(1)}, u32[]{:S(2)}, u32[]{:S(2)}) %collective-permute-start.21) | collective-permute-done | bytes 147488 | tf_op jit(solution)/shard_map/ppermute | solution.py:52
  208.1 0.3 fusion.43
  208.4 0.1 collective-permute-start.22
  208.5 1.2 collective-permute-done.22
  209.8 0.6 collective-permute-start.23
  210.3 0.3 fusion.47
  210.7 1.2 collective-permute-done.25
  211.9 1.5 collective-permute-start.26
  213.4 2.3 %collective-permute-done.23 = bf16[64,1024]{1,0:T(8,128)(2,1)S(1)} collective-permute-done((bf16[64,1024]{1,0:T(8,128)(2,1)S(1)}, bf16[64,1024]{1,0:T(8,128)(2,1)S(1)}, u32[]{:S(2)}, u32[]{:S(2)}) %collective-permute-start.23) | collective-permute-done | bytes 131104 | tf_op jit(solution)/shard_map/ppermute | solution.py:61
  215.9 0.2 collective-permute-done.26
  216.1 3.4 %collective-permute-start.27 = (f32[64,64]{1,0:T(8,128)S(1)}, f32[64,64]{1,0:T(8,128)S(1)}, u32[]{:S(2)}, u32[]{:S(2)}) collective-permute-start(f32[64,64]{1,0:T(8,128)S(1)} %add.207), channel_id=1, source_target_pairs={{0,4},{1,5},{2,6},{3,7},{4,0},{5,1},{6,2},{7,3},{8,12},{9,13},{10,... | collective-permute-start | bytes 49160 | tf_op jit(solution)/shard_map/ppermute | solution.py:61
  219.6 5.8 %collective-permute-done.27 = f32[64,64]{1,0:T(8,128)S(1)} collective-permute-done((f32[64,64]{1,0:T(8,128)S(1)}, f32[64,64]{1,0:T(8,128)S(1)}, u32[]{:S(2)}, u32[]{:S(2)}) %collective-permute-start.27) | collective-permute-done | bytes 16416 | tf_op jit(solution)/shard_map/ppermute | solution.py:61
  225.3 0.4 convolution_add_fusion
  225.8 2.3 %fusion.11 = f32[1024,64]{0,1:T(8,128)} fusion(f32[1024,64]{0,1:T(8,128)S(1)} %convolution_add_fusion, f32[1024,64]{0,1:T(8,128)S(1)} %fusion.12, bf16[1024,4096]{0,1:T(8,128)(2,1)S(1)} %bitcast.28, bf16[64,2048]{1,0:T(8,128)(2,1)S(1)} %maximum_select_fusion.5, bf16[64,2048]{1,0:T(8,128)(2,1)S(1)} %collective-permute-done.24, pred[]{:T(512)S(6)} %eq.71), kind=kOutput, calls=%fused_computation.18 | convolution fusion | flops 539361280 | bytes 9699329 | tf_op jit(solution)/shard_map/dot_general | solution.py:121
  (62 shorter events, 1.5 us)
Async XLA Ops:
  24.2 18.4 %copy-start = (f32[1024,64]{0,1:T(8,128)S(1)}, f32[1024,64]{0,1:T(8,128)}, u32[]{:S(2)}) copy-start(f32[1024,64]{0,1:T(8,128)} %param.8) | copy-start | bytes 786436
  42.6 74.5 %copy-start.2 = (f32[64,512]{1,0:T(8,128)S(1)}, f32[64,512]{1,0:T(8,128)}, u32[]{:S(2)}) copy-start(f32[64,512]{1,0:T(8,128)} %param.9) | copy-start | bytes 393220
  49.2 15.9 %collective-permute-start = (f32[64,2112]{1,0:T(8,128)S(1)}, f32[64,2112]{1,0:T(8,128)S(1)}, u32[]{:S(2)}, u32[]{:S(2)}) collective-permute-start(f32[64,2112]{1,0:T(8,128)S(1)} %pad_maximum_fusion), channel_id=1, source_target_pairs={{0,4},{1,5},{2,6},{3,7},{4,0},{5,1},{6,2},{7,3},{8,12},{9,13},{10,... | collective-permute-start | bytes 1622024 | tf_op jit(solution)/shard_map/ppermute | solution.py:42
  65.2 8.0 %collective-permute-start.1 = (f32[64,1088]{1,0:T(8,128)S(1)}, f32[64,1088]{1,0:T(8,128)S(1)}, u32[]{:S(2)}, u32[]{:S(2)}) collective-permute-start(f32[64,1088]{1,0:T(8,128)S(1)} %pad_maximum_fusion.2), channel_id=1, source_target_pairs={{0,2},{1,3},{2,0},{3,1},{4,6},{5,7},{6,4},{7,5},{8,10},{9,11},{10,... | collective-permute-start | bytes 835592 | tf_op jit(solution)/shard_map/ppermute | solution.py:42
  73.3 1.5 collective-permute-start.2
  74.8 6.3 %collective-permute-start.3 = (f32[64,576]{1,0:T(8,128)S(1)}, f32[64,576]{1,0:T(8,128)S(1)}, u32[]{:S(2)}, u32[]{:S(2)}) collective-permute-start(f32[64,576]{1,0:T(8,128)S(1)} %pad_maximum_fusion.5), channel_id=1, source_target_pairs={{0,8},{8,0},{16,24},{24,16},{32,40},{40,32},{48,56},{56,48},{64,72... | collective-permute-start | bytes 442376 | tf_op jit(solution)/shard_map/ppermute | solution.py:52
  81.2 7.0 %collective-permute-start.4 = (f32[64,576]{1,0:T(8,128)S(1)}, f32[64,576]{1,0:T(8,128)S(1)}, u32[]{:S(2)}, u32[]{:S(2)}) collective-permute-start(f32[64,576]{1,0:T(8,128)S(1)} %fusion.41), channel_id=1, source_target_pairs={{0,16},{8,24},{16,0},{24,8},{32,48},{40,56},{48,32},{56,40},{64,80... | collective-permute-start | bytes 442376 | tf_op jit(solution)/shard_map/ppermute | solution.py:52
  88.2 5.6 %collective-permute-start.5 = (f32[64,576]{1,0:T(8,128)S(1)}, f32[64,576]{1,0:T(8,128)S(1)}, u32[]{:S(2)}, u32[]{:S(2)}) collective-permute-start(f32[64,576]{1,0:T(8,128)S(1)} %add.184), channel_id=1, source_target_pairs={{0,32},{8,40},{16,48},{24,56},{32,0},{40,8},{48,16},{56,24},{64,96... | collective-permute-start | bytes 442376 | tf_op jit(solution)/shard_map/ppermute | solution.py:52
  93.8 8.7 %collective-permute-start.6 = (f32[64,576]{1,0:T(8,128)S(1)}, f32[64,576]{1,0:T(8,128)S(1)}, u32[]{:S(2)}, u32[]{:S(2)}) collective-permute-start(f32[64,576]{1,0:T(8,128)S(1)} %add.185), channel_id=1, source_target_pairs={{0,64},{8,72},{16,80},{24,88},{32,96},{40,104},{48,112},{56,120},{... | collective-permute-start | bytes 442376 | tf_op jit(solution)/shard_map/ppermute | solution.py:52
  102.5 14.6 %collective-permute-start.7 = (f32[64,576]{1,0:T(8,128)S(1)}, f32[64,576]{1,0:T(8,128)S(1)}, u32[]{:S(2)}, u32[]{:S(2)}) collective-permute-start(f32[64,576]{1,0:T(8,128)S(1)} %add.186), channel_id=1, source_target_pairs={{0,128},{8,136},{16,144},{24,152},{32,160},{40,168},{48,176},{56,1... | collective-permute-start | bytes 442376 | tf_op jit(solution)/shard_map/ppermute | solution.py:52
  117.4 1.3 collective-permute-start.8
  118.8 5.6 %collective-permute-start.9 = (bf16[64,1024]{1,0:T(8,128)(2,1)S(1)}, bf16[64,1024]{1,0:T(8,128)(2,1)S(1)}, u32[]{:S(2)}, u32[]{:S(2)}) collective-permute-start(bf16[64,1024]{1,0:T(8,128)(2,1)S(1)} %maximum_select_fusion.6), channel_id=1, source_target_pairs={{0,2},{1,3},{2,0},{3,1},{4,6},{5,7},{6,4},{7,5},{8,10},{9,11},{10,... | collective-permute-start | bytes 393224 | tf_op jit(solution)/shard_map/ppermute | solution.py:61
  120.4 1.3 collective-permute-start.11
  121.7 3.9 %collective-permute-start.12 = (f32[64,64]{1,0:T(8,128)S(1)}, f32[64,64]{1,0:T(8,128)S(1)}, u32[]{:S(2)}, u32[]{:S(2)}) collective-permute-start(f32[64,64]{1,0:T(8,128)S(1)} %add.189), channel_id=1, source_target_pairs={{0,2},{1,3},{2,0},{3,1},{4,6},{5,7},{6,4},{7,5},{8,10},{9,11},{10,... | collective-permute-start | bytes 49160 | tf_op jit(solution)/shard_map/ppermute | solution.py:61
  124.5 10.3 %collective-permute-start.10 = (bf16[64,2048]{1,0:T(8,128)(2,1)S(1)}, bf16[64,2048]{1,0:T(8,128)(2,1)S(1)}, u32[]{:S(2)}, u32[]{:S(2)}) collective-permute-start(bf16[64,2048]{1,0:T(8,128)(2,1)S(1)} %maximum_select_fusion.4), channel_id=1, source_target_pairs={{0,4},{1,5},{2,6},{3,7},{4,0},{5,1},{6,2},{7,3},{8,12},{9,13},{10,... | collective-permute-start | bytes 786440 | tf_op jit(solution)/shard_map/ppermute | solution.py:61
  125.6 8.7 %collective-permute-start.13 = (f32[64,64]{1,0:T(8,128)S(1)}, f32[64,64]{1,0:T(8,128)S(1)}, u32[]{:S(2)}, u32[]{:S(2)}) collective-permute-start(f32[64,64]{1,0:T(8,128)S(1)} %add.190), channel_id=1, source_target_pairs={{0,4},{1,5},{2,6},{3,7},{4,0},{5,1},{6,2},{7,3},{8,12},{9,13},{10,... | collective-permute-start | bytes 49160 | tf_op jit(solution)/shard_map/ppermute | solution.py:61
  134.7 91.0 %slice-start = ((s8[8388608]{0:T(1024)(128)(4,1)}), s8[4194304]{0:T(1024)(128)(4,1)S(1)}, s32[]{:S(2)}) async-start(s8[8388608]{0:T(1024)(128)(4,1)} %bitcast.26), calls=%async_computation | async-start | bytes 8388608
  139.9 85.9 %slice-start.1 = ((s8[8388608]{0:T(1024)(128)(4,1)}), s8[4194304]{0:T(1024)(128)(4,1)S(1)}, s32[]{:S(2)}) async-start(s8[8388608]{0:T(1024)(128)(4,1)} %bitcast.26), calls=%async_computation.1 | async-start | bytes 8388608
  146.6 15.0 %collective-permute-start.14 = (f32[64,2112]{1,0:T(8,128)S(1)}, f32[64,2112]{1,0:T(8,128)S(1)}, u32[]{:S(2)}, u32[]{:S(2)}) collective-permute-start(f32[64,2112]{1,0:T(8,128)S(1)} %pad_maximum_fusion.1), channel_id=1, source_target_pairs={{0,4},{1,5},{2,6},{3,7},{4,0},{5,1},{6,2},{7,3},{8,12},{9,13},{10,... | collective-permute-start | bytes 1622024 | tf_op jit(solution)/shard_map/ppermute | solution.py:42
  161.7 6.8 %collective-permute-start.15 = (f32[64,1088]{1,0:T(8,128)S(1)}, f32[64,1088]{1,0:T(8,128)S(1)}, u32[]{:S(2)}, u32[]{:S(2)}) collective-permute-start(f32[64,1088]{1,0:T(8,128)S(1)} %pad_maximum_fusion.3), channel_id=1, source_target_pairs={{0,2},{1,3},{2,0},{3,1},{4,6},{5,7},{6,4},{7,5},{8,10},{9,11},{10,... | collective-permute-start | bytes 835592 | tf_op jit(solution)/shard_map/ppermute | solution.py:42
  168.6 1.5 collective-permute-start.16
  170.1 6.3 %collective-permute-start.17 = (f32[64,576]{1,0:T(8,128)S(1)}, f32[64,576]{1,0:T(8,128)S(1)}, u32[]{:S(2)}, u32[]{:S(2)}) collective-permute-start(f32[64,576]{1,0:T(8,128)S(1)} %pad_maximum_fusion.7), channel_id=1, source_target_pairs={{0,8},{8,0},{16,24},{24,16},{32,40},{40,32},{48,56},{56,48},{64,72... | collective-permute-start | bytes 442376 | tf_op jit(solution)/shard_map/ppermute | solution.py:52
  176.5 7.2 %collective-permute-start.18 = (f32[64,576]{1,0:T(8,128)S(1)}, f32[64,576]{1,0:T(8,128)S(1)}, u32[]{:S(2)}, u32[]{:S(2)}) collective-permute-start(f32[64,576]{1,0:T(8,128)S(1)} %fusion.40), channel_id=1, source_target_pairs={{0,16},{8,24},{16,0},{24,8},{32,48},{40,56},{48,32},{56,40},{64,80... | collective-permute-start | bytes 442376 | tf_op jit(solution)/shard_map/ppermute | solution.py:52
  183.7 5.4 %collective-permute-start.19 = (f32[64,576]{1,0:T(8,128)S(1)}, f32[64,576]{1,0:T(8,128)S(1)}, u32[]{:S(2)}, u32[]{:S(2)}) collective-permute-start(f32[64,576]{1,0:T(8,128)S(1)} %add.201), channel_id=1, source_target_pairs={{0,32},{8,40},{16,48},{24,56},{32,0},{40,8},{48,16},{56,24},{64,96... | collective-permute-start | bytes 442376 | tf_op jit(solution)/shard_map/ppermute | solution.py:52
  189.2 7.8 %collective-permute-start.20 = (f32[64,576]{1,0:T(8,128)S(1)}, f32[64,576]{1,0:T(8,128)S(1)}, u32[]{:S(2)}, u32[]{:S(2)}) collective-permute-start(f32[64,576]{1,0:T(8,128)S(1)} %add.202), channel_id=1, source_target_pairs={{0,64},{8,72},{16,80},{24,88},{32,96},{40,104},{48,112},{56,120},{... | collective-permute-start | bytes 442376 | tf_op jit(solution)/shard_map/ppermute | solution.py:52
  197.0 11.1 %collective-permute-start.21 = (f32[64,576]{1,0:T(8,128)S(1)}, f32[64,576]{1,0:T(8,128)S(1)}, u32[]{:S(2)}, u32[]{:S(2)}) collective-permute-start(f32[64,576]{1,0:T(8,128)S(1)} %add.203), channel_id=1, source_target_pairs={{0,128},{8,136},{16,144},{24,152},{32,160},{40,168},{48,176},{56,1... | collective-permute-start | bytes 442376 | tf_op jit(solution)/shard_map/ppermute | solution.py:52
  208.4 19.7 %copy-start.1 = (f32[64,512]{1,0:T(8,128)}, f32[64,512]{1,0:T(8,128)S(1)}, u32[]{:S(2)}) copy-start(f32[64,512]{1,0:T(8,128)S(1)} %get-tuple-element.22) | copy-start | bytes 393220
  208.4 1.3 collective-permute-start.22
  209.8 6.0 %collective-permute-start.23 = (bf16[64,1024]{1,0:T(8,128)(2,1)S(1)}, bf16[64,1024]{1,0:T(8,128)(2,1)S(1)}, u32[]{:S(2)}, u32[]{:S(2)}) collective-permute-start(bf16[64,1024]{1,0:T(8,128)(2,1)S(1)} %maximum_select_fusion.7), channel_id=1, source_target_pairs={{0,2},{1,3},{2,0},{3,1},{4,6},{5,7},{6,4},{7,5},{8,10},{9,11},{10,... | collective-permute-start | bytes 393224 | tf_op jit(solution)/shard_map/ppermute | solution.py:61
  210.6 1.3 collective-permute-start.25
  211.9 4.2 %collective-permute-start.26 = (f32[64,64]{1,0:T(8,128)S(1)}, f32[64,64]{1,0:T(8,128)S(1)}, u32[]{:S(2)}, u32[]{:S(2)}) collective-permute-start(f32[64,64]{1,0:T(8,128)S(1)} %add.206), channel_id=1, source_target_pairs={{0,2},{1,3},{2,0},{3,1},{4,6},{5,7},{6,4},{7,5},{8,10},{9,11},{10,... | collective-permute-start | bytes 49160 | tf_op jit(solution)/shard_map/ppermute | solution.py:61
  215.8 9.9 %collective-permute-start.24 = (bf16[64,2048]{1,0:T(8,128)(2,1)S(1)}, bf16[64,2048]{1,0:T(8,128)(2,1)S(1)}, u32[]{:S(2)}, u32[]{:S(2)}) collective-permute-start(bf16[64,2048]{1,0:T(8,128)(2,1)S(1)} %maximum_select_fusion.5), channel_id=1, source_target_pairs={{0,4},{1,5},{2,6},{3,7},{4,0},{5,1},{6,2},{7,3},{8,12},{9,13},{10,... | collective-permute-start | bytes 786440 | tf_op jit(solution)/shard_map/ppermute | solution.py:61
  216.1 9.2 %collective-permute-start.27 = (f32[64,64]{1,0:T(8,128)S(1)}, f32[64,64]{1,0:T(8,128)S(1)}, u32[]{:S(2)}, u32[]{:S(2)}) collective-permute-start(f32[64,64]{1,0:T(8,128)S(1)} %add.207), channel_id=1, source_target_pairs={{0,4},{1,5},{2,6},{3,7},{4,0},{5,1},{6,2},{7,3},{8,12},{9,13},{10,... | collective-permute-start | bytes 49160 | tf_op jit(solution)/shard_map/ppermute | solution.py:61

commit v3 on v2

--- a/solution.py
+++ b/solution.py
@@ -31,27 +31,29 @@
     return [(i, i ^ s) for i in range(n)]
 
 
-def halve_scatter(x, g, axis, n):
+def scatter_once(x, g, axis, n):
     j = lax.axis_index(axis)
-    s = n // 2
-    while s >= 1:
-        half = x.shape[1] // 2
-        bit = (j // s) % 2
-        keep = lax.dynamic_slice_in_dim(x, bit * half, half, axis=1)
-        send = lax.dynamic_slice_in_dim(x, (1 - bit) * half, half, axis=1)
-        got = lax.ppermute(jnp.concatenate([send, g], axis=1), axis, pairs(n, s))
-        x = keep + got[:, :half]
-        g = g + got[:, half:]
-        s //= 2
-    return x, g
+    w = x.shape[1] // n
+    acc = jnp.concatenate([lax.dynamic_slice_in_dim(x, j * w, w, axis=1), g], axis=1)
+    for t in range(1, n):
+        send = jnp.concatenate([lax.dynamic_slice_in_dim(x, ((j + t) % n) * w, w, axis=1), g], axis=1)
+        acc = acc + lax.ppermute(send, axis, [(i, (i + t) % n) for i in range(n)])
+    return acc[:, :w], acc[:, w:]
 
 
-def double_sum(x, axis, n):
-    s = 1
+def halve_sum(x, axis, n):
+    j = lax.axis_index(axis)
+    half = x.shape[1] // 2
+    bit = j % 2
+    keep = lax.dynamic_slice_in_dim(x, bit * half, half, axis=1)
+    send = lax.dynamic_slice_in_dim(x, (1 - bit) * half, half, axis=1)
+    x = keep + lax.ppermute(send, axis, pairs(n, 1))
+    s = 2
     while s < n:
         x = x + lax.ppermute(x, axis, pairs(n, s))
         s *= 2
-    return x
+    other = lax.ppermute(x, axis, pairs(n, 1))
+    return jnp.where(bit == 1, jnp.concatenate([other, x], axis=1), jnp.concatenate([x, other], axis=1))
 
 
 def double_gather(x, g, axis, n):
@@ -83,7 +85,8 @@
     spectra = spectra.reshape(rows, MZ * MOB)
     highest = lax.Precision.HIGHEST
     basis, profiles = (basis_init, profile_init)
-    for step in range(ITERS):
+    def round_(step, carry):
+        basis, profiles = carry
         partial_h = lax.dot_general(
             basis.astype(jnp.bfloat16),
             spectra,
@@ -97,8 +100,8 @@
             precision=highest,
             preferred_element_type=jnp.float32,
         )
-        shared, gram_feat = halve_scatter(partial_h, partial_gram, "feat", n_feat)
-        both = double_sum(jnp.concatenate([shared, gram_feat], axis=1), "pix", n_pix)
+        shared, gram_feat = scatter_once(partial_h, partial_gram, "feat", n_feat)
+        both = halve_sum(jnp.concatenate([shared, gram_feat], axis=1), "pix", n_pix)
         width = shared.shape[1]
         numer_h = both[:, :width]
         gram_w = both[:, width:]
@@ -129,6 +132,9 @@
             * numer_w
             / (jnp.dot(basis, gram_h, precision=highest, preferred_element_type=jnp.float32) + EPS)
         )
+        return (basis, profiles)
+
+    basis, profiles = lax.fori_loop(0, ITERS, round_, (basis, profiles))
     return (basis, profiles)
 
 

time: 229 us -> 241 us (1.052); the launches traced: 228 us -> 236 us
  waiting for transfers between devices: 114 us -> 89 us
  starting transfers between devices: 47.7 us -> 65.8 us
  local copies, waits for them, and re-layouts: 18.6 us -> 30.8 us
    ppermute x16 -> x26, waiting for transfers between devices: 92.1 us -> 66.6 us  [the longest x8 28.4 us: halve_sum(): x = x + lax.ppermute(x, axis, pairs(n, s))]
    ppermute x16 -> x26, starting transfers between devices: 36.6 us -> 50 us  [the longest x8 29.9 us: halve_sum(): x = x + lax.ppermute(x, axis, pairs(n, s))]
    while x0 -> x5, local copies, waits for them, and re-layouts: none -> 11.3 us  [the longest x1 11.2 us: local(): basis, profiles = lax.fori_loop(0, ITERS, round_, (basis, profiles))]
    ppermute x12, starting transfers between devices: 11.1 us -> 15.8 us  [double_gather(): other, got_g = lax.ppermute((x, g), axis, pairs(n, s))]
  transfers between devices with their start and end apart: 28 -> 38, of which waited for: 26 -> 31; matrix products, arithmetic and copies ran while one was open for 1% -> 5% of each run, Pallas kernels for 0% -> 0%
where the time goes in v3:
time: 241 us; the launch traced here: 236 us
  waiting for transfers between devices  89 us (37%)
  starting transfers between devices  65.8 us (27%)
  matrix products  45.7 us (19%)
  local copies, waits for them, and re-layouts  30.8 us (13%)
  other arithmetic  3.55 us (1%)
    ppermute x8, starting transfers between devices, halve_sum(): x = x + lax.ppermute(x, axis, pairs(n, s))  29.9 us
    ppermute x8, waiting for transfers between devices, halve_sum(): x = x + lax.ppermute(x, axis, pairs(n, s))  28.4 us
    ppermute x14, waiting for transfers between devices, scatter_once(): acc = acc + lax.ppermute(send, axis, [(i, (i + t) % n) for i in range(n)])  25.2 us
    ppermute x12, waiting for transfers between devices, double_gather(): other, got_g = lax.ppermute((x, g), axis, pairs(n, s))  22.4 us
    dot_general x1, matrix products, bin_block(): jnp.einsum('pkh,pkl->phl', hi_hot, lo_hot, preferred_element_type=jnp.flo...  21.1 us
    convert_element_type x1, local copies, waits for them, and re-layouts, bin_block(): return dense.reshape(mass.shape[0], MZ * MOB).astype(jnp.bfloat16)  18.4 us
    ppermute x12, starting transfers between devices, double_gather(): other, got_g = lax.ppermute((x, g), axis, pairs(n, s))  15.8 us
    ppermute x14, starting transfers between devices, scatter_once(): acc = acc + lax.ppermute(send, axis, [(i, (i + t) % n) for i in range(n)])  14.2 us
  transfers between devices with their start and end apart: 38, of which 31 were waited for; matrix products, arithmetic and copies ran while one was open for 5% of the time, Pallas kernels for 0%

profile of v3, /device:TPU:16, one launch (start us, length us, event | category | flops | bytes accessed | tf_op | source)
XLA Modules:
  0.0 236.0 jit_solution(5516448733553995348)
XLA Ops:
  0.6 2.5 %add_select_fusion.1 = (s32[1024,256]{1,0:T(8,128)S(1)}, s32[1024,256]{1,0:T(8,128)S(1)}) fusion(s32[1024,256]{1,0:T(8,128)} %param.7, s32[1024,256]{1,0:T(8,128)} %param.8), kind=kLoop, calls=%fused_computation.58 | loop fusion | flops 5505024 | bytes 4194304 | tf_op jit(solution)/shard_map/while/body/eval_jaxpr/jit(floor_divide)/jit(_where)/select_n | solution.py:21
  3.1 21.1 %fusion.29 = bf16[1024,64,64]{2,1,0:T(8,128)(2,1)} fusion(s32[1024,256]{1,0:T(8,128)S(1)} %get-tuple-element.140, s32[1024,256]{1,0:T(8,128)S(1)} %get-tuple-element.139, bf16[1024,256]{1,0:T(8,128)(2,1)} %param.9), kind=kOutput, calls=%fused_computation.56 | convolution fusion | flops 2202009600 | bytes 11010048 | tf_op jit(solution)/shard_map/while/body/eval_jaxpr/pkh,pkl->phl/dot_general | solution.py:26
  24.2 18.4 %copy.7 = bf16[1024,64,64]{0,2,1:T(8,128)(2,1)} copy(bf16[1024,64,64]{2,1,0:T(8,128)(2,1)} %fusion.29) | data formatting | bytes 16777216 | tf_op jit(solution)/shard_map/while/body/eval_jaxpr/convert_element_type | solution.py:27
  42.6 11.2 %copy.8 = bf16[1024,4096]{1,0:T(8,128)(2,1)} copy(bf16[1024,4096]{0,1:T(8,128)(2,1)} %bitcast.37) | data formatting | bytes 16777216 | tf_op jit(solution)/shard_map/while | solution.py:137
  53.9 181.4 %while.19 = (s32[]{:T(128)}, f32[1024,64]{0,1:T(8,128)S(1)}, f32[64,512]{1,0:T(8,128)S(1)}, bf16[1024,4096]{1,0:T(8,128)(2,1)}, s32[]{:T(128)}, /*index=5*/u32[]...) while((s32[]{:T(128)}, f32[1024,64]{0,1:T(8,128)S(1)}, ...), condition=%wide.region_1.2_spmd, body=%wide.region_0.1_spmd.sunk | while | flops 1230026752 | bytes 37546916 | solution.py:137
  54.3 4.9 %fusion.74 = f32[64,4096]{1,0:T(8,128)S(1)} fusion(bf16[1024,4096]{1,0:T(8,128)(2,1)} %get-tuple-element.245, f32[1024,64]{0,1:T(8,128)S(1)} %copy.24), kind=kOutput, calls=%fused_computation.33.clone.1 | convolution fusion | flops 536936448 | bytes 9699328 | tf_op jit(solution)/shard_map/while/body/eval_jaxpr/dot_general | solution.py:90
  60.0 2.6 %collective-permute-start.2 = (f32[64,576]{1,0:T(8,128)S(1)}, f32[64,576]{1,0:T(8,128)S(1)}, u32[]{:S(2)}, u32[]{:S(2)}) collective-permute-start(f32[64,576]{1,0:T(8,128)S(1)} %get-tuple-element.192), channel_id=1, source_target_pairs={{0,5},{1,6},{2,7},{3,0},{4,1},{5,2},{6,3},{7,4},{8,13},{9,14},{10,... | collective-permute-start | bytes 442376 | tf_op jit(solution)/shard_map/while/body/eval_jaxpr/ppermute | solution.py:40
  62.7 0.6 collective-permute-start.3
  63.3 1.8 collective-permute-start.4
  65.1 1.9 collective-permute-start.5
  67.0 2.4 %collective-permute-done.1 = f32[64,576]{1,0:T(8,128)S(1)} collective-permute-done((f32[64,576]{1,0:T(8,128)S(1)}, f32[64,576]{1,0:T(8,128)S(1)}, u32[]{:S(2)}, u32[]{:S(2)}) %collective-permute-start.1) | collective-permute-done | bytes 147488 | tf_op jit(solution)/shard_map/while/body/eval_jaxpr/ppermute | solution.py:40
  69.6 1.7 collective-permute-done.3
  71.3 2.9 %collective-permute-done.4 = f32[64,576]{1,0:T(8,128)S(1)} collective-permute-done((f32[64,576]{1,0:T(8,128)S(1)}, f32[64,576]{1,0:T(8,128)S(1)}, u32[]{:S(2)}, u32[]{:S(2)}) %collective-permute-start.4) | collective-permute-done | bytes 147488 | tf_op jit(solution)/shard_map/while/body/eval_jaxpr/ppermute | solution.py:40
  74.2 5.0 %collective-permute-done.5 = f32[64,576]{1,0:T(8,128)S(1)} collective-permute-done((f32[64,576]{1,0:T(8,128)S(1)}, f32[64,576]{1,0:T(8,128)S(1)}, u32[]{:S(2)}, u32[]{:S(2)}) %collective-permute-start.5) | collective-permute-done | bytes 147488 | tf_op jit(solution)/shard_map/while/body/eval_jaxpr/ppermute | solution.py:40
  79.5 1.2 collective-permute-start.7
  80.7 3.5 %collective-permute-done.7 = f32[64,288]{1,0:T(8,128)S(1)} collective-permute-done((f32[64,288]{1,0:T(8,128)S(1)}, f32[64,288]{1,0:T(8,128)S(1)}, u32[]{:S(2)}, u32[]{:S(2)}) %collective-permute-start.7) | collective-permute-done | bytes 73760 | tf_op jit(solution)/shard_map/while/body/eval_jaxpr/ppermute | solution.py:50
  84.3 2.7 %collective-permute-start.8 = (f32[64,288]{1,0:T(8,128)S(1)}, f32[64,288]{1,0:T(8,128)S(1)}, u32[]{:S(2)}, u32[]{:S(2)}) collective-permute-start(f32[64,288]{1,0:T(8,128)S(1)} %dynamic-slice_add_fusion.2), channel_id=1, source_target_pairs={{0,16},{8,24},{16,0},{24,8},{32,48},{40,56},{48,32},{56,40},{64,80... | collective-permute-start | bytes 221192 | tf_op jit(solution)/shard_map/while/body/eval_jaxpr/ppermute | solution.py:53
  87.1 4.4 %collective-permute-done.8 = f32[64,288]{1,0:T(8,128)S(1)} collective-permute-done((f32[64,288]{1,0:T(8,128)S(1)}, f32[64,288]{1,0:T(8,128)S(1)}, u32[]{:S(2)}, u32[]{:S(2)}) %collective-permute-start.8) | collective-permute-done | bytes 73760 | tf_op jit(solution)/shard_map/while/body/eval_jaxpr/ppermute | solution.py:53
  91.5 1.5 collective-permute-start.9
  93.0 3.3 %collective-permute-done.9 = f32[64,288]{1,0:T(8,128)S(1)} collective-permute-done((f32[64,288]{1,0:T(8,128)S(1)}, f32[64,288]{1,0:T(8,128)S(1)}, u32[]{:S(2)}, u32[]{:S(2)}) %collective-permute-start.9) | collective-permute-done | bytes 73760 | tf_op jit(solution)/shard_map/while/body/eval_jaxpr/ppermute | solution.py:53
  96.3 3.2 %collective-permute-start.10 = (f32[64,288]{1,0:T(8,128)S(1)}, f32[64,288]{1,0:T(8,128)S(1)}, u32[]{:S(2)}, u32[]{:S(2)}) collective-permute-start(f32[64,288]{1,0:T(8,128)S(1)} %add.511), channel_id=1, source_target_pairs={{0,64},{8,72},{16,80},{24,88},{32,96},{40,104},{48,112},{56,120},{... | collective-permute-start | bytes 221192 | tf_op jit(solution)/shard_map/while/body/eval_jaxpr/ppermute | solution.py:53
  99.4 4.5 %collective-permute-done.10 = f32[64,288]{1,0:T(8,128)S(1)} collective-permute-done((f32[64,288]{1,0:T(8,128)S(1)}, f32[64,288]{1,0:T(8,128)S(1)}, u32[]{:S(2)}, u32[]{:S(2)}) %collective-permute-start.10) | collective-permute-done | bytes 73760 | tf_op jit(solution)/shard_map/while/body/eval_jaxpr/ppermute | solution.py:53
  104.0 6.3 %collective-permute-start.11 = (f32[64,288]{1,0:T(8,128)S(1)}, f32[64,288]{1,0:T(8,128)S(1)}, u32[]{:S(2)}, u32[]{:S(2)}) collective-permute-start(f32[64,288]{1,0:T(8,128)S(1)} %add.512), channel_id=1, source_target_pairs={{0,128},{8,136},{16,144},{24,152},{32,160},{40,168},{48,176},{56,1... | collective-permute-start | bytes 221192 | tf_op jit(solution)/shard_map/while/body/eval_jaxpr/ppermute | solution.py:53
  110.3 3.6 %collective-permute-done.11 = f32[64,288]{1,0:T(8,128)S(1)} collective-permute-done((f32[64,288]{1,0:T(8,128)S(1)}, f32[64,288]{1,0:T(8,128)S(1)}, u32[]{:S(2)}, u32[]{:S(2)}) %collective-permute-start.11) | collective-permute-done | bytes 73760 | tf_op jit(solution)/shard_map/while/body/eval_jaxpr/ppermute | solution.py:53
  114.0 1.6 collective-permute-start.12
  115.5 3.1 %collective-permute-done.12 = f32[64,288]{1,0:T(8,128)S(1)} collective-permute-done((f32[64,288]{1,0:T(8,128)S(1)}, f32[64,288]{1,0:T(8,128)S(1)}, u32[]{:S(2)}, u32[]{:S(2)}) %collective-permute-start.12) | collective-permute-done | bytes 73760 | tf_op jit(solution)/shard_map/while/body/eval_jaxpr/ppermute | solution.py:55
  119.2 1.2 collective-permute-done.13
  120.4 3.8 %collective-permute-start.14 = (bf16[64,1024]{1,0:T(8,128)(2,1)S(1)}, bf16[64,1024]{1,0:T(8,128)(2,1)S(1)}, u32[]{:S(2)}, u32[]{:S(2)}) collective-permute-start(bf16[64,1024]{1,0:T(8,128)(2,1)S(1)} %maximum_select_fusion.11), channel_id=1, source_target_pairs={{0,2},{1,3},{2,0},{3,1},{4,6},{5,7},{6,4},{7,5},{8,10},{9,11},{10,... | collective-permute-start | bytes 393224 | tf_op jit(solution)/shard_map/while/body/eval_jaxpr/ppermute | solution.py:63
  124.2 3.8 %collective-permute-done.14 = bf16[64,1024]{1,0:T(8,128)(2,1)S(1)} collective-permute-done((bf16[64,1024]{1,0:T(8,128)(2,1)S(1)}, bf16[64,1024]{1,0:T(8,128)(2,1)S(1)}, u32[]{:S(2)}, u32[]{:S(2)}) %collective-permute-start.14) | collective-permute-done | bytes 131104 | tf_op jit(solution)/shard_map/while/body/eval_jaxpr/ppermute | solution.py:63
  128.1 1.5 collective-permute-start.15
  130.0 1.2 collective-permute-done.16
  131.2 0.9 collective-permute-start.17
  132.1 5.0 %collective-permute-done.17 = f32[64,64]{1,0:T(8,128)S(1)} collective-permute-done((f32[64,64]{1,0:T(8,128)S(1)}, f32[64,64]{1,0:T(8,128)S(1)}, u32[]{:S(2)}, u32[]{:S(2)}) %collective-permute-start.17) | collective-permute-done | bytes 16416 | tf_op jit(solution)/shard_map/while/body/eval_jaxpr/ppermute | solution.py:63
  137.1 2.0 collective-permute-start.18
  139.1 6.0 %fusion.77 = f32[1024,64]{0,1:T(8,128)S(1)} fusion(f32[1024,64]{0,1:T(8,128)S(1)} %copy.24, bf16[1024,4096]{1,0:T(8,128)(2,1)} %get-tuple-element.245, bf16[64,2048]{1,0:T(8,128)(2,1)S(1)} %maximum_select_fusion.12, bf16[64,2048]{1,0:T(8,128)(2,1)S(1)} %collective-permute-done.15, pred[]{:T(512)S(6)} %eq.129), kind=kOutput, calls=%fused_computation.4.clone.1 | convolution fusion | flops 539295744 | bytes 9437185 | tf_op jit(solution)/shard_map/while/body/eval_jaxpr/dot_general | solution.py:124
  146.1 4.9 %fusion.74 = f32[64,4096]{1,0:T(8,128)S(1)} fusion(bf16[1024,4096]{1,0:T(8,128)(2,1)} %get-tuple-element.245, f32[1024,64]{0,1:T(8,128)S(1)} %copy.24), kind=kOutput, calls=%fused_computation.33.clone.1 | convolution fusion | flops 536936448 | bytes 9699328 | tf_op jit(solution)/shard_map/while/body/eval_jaxpr/dot_general | solution.py:90
  151.7 3.4 %collective-permute-start.2 = (f32[64,576]{1,0:T(8,128)S(1)}, f32[64,576]{1,0:T(8,128)S(1)}, u32[]{:S(2)}, u32[]{:S(2)}) collective-permute-start(f32[64,576]{1,0:T(8,128)S(1)} %get-tuple-element.192), channel_id=1, source_target_pairs={{0,5},{1,6},{2,7},{3,0},{4,1},{5,2},{6,3},{7,4},{8,13},{9,14},{10,... | collective-permute-start | bytes 442376 | tf_op jit(solution)/shard_map/while/body/eval_jaxpr/ppermute | solution.py:40
  155.3 2.1 collective-permute-start.4
  157.4 0.6 collective-permute-start.5
  158.0 3.7 %collective-permute-done.1 = f32[64,576]{1,0:T(8,128)S(1)} collective-permute-done((f32[64,576]{1,0:T(8,128)S(1)}, f32[64,576]{1,0:T(8,128)S(1)}, u32[]{:S(2)}, u32[]{:S(2)}) %collective-permute-start.1) | collective-permute-done | bytes 147488 | tf_op jit(solution)/shard_map/while/body/eval_jaxpr/ppermute | solution.py:40
  161.7 2.1 collective-permute-done.3
  163.8 2.6 %collective-permute-done.4 = f32[64,576]{1,0:T(8,128)S(1)} collective-permute-done((f32[64,576]{1,0:T(8,128)S(1)}, f32[64,576]{1,0:T(8,128)S(1)}, u32[]{:S(2)}, u32[]{:S(2)}) %collective-permute-start.4) | collective-permute-done | bytes 147488 | tf_op jit(solution)/shard_map/while/body/eval_jaxpr/ppermute | solution.py:40
  166.4 4.4 %collective-permute-done.5 = f32[64,576]{1,0:T(8,128)S(1)} collective-permute-done((f32[64,576]{1,0:T(8,128)S(1)}, f32[64,576]{1,0:T(8,128)S(1)}, u32[]{:S(2)}, u32[]{:S(2)}) %collective-permute-start.5) | collective-permute-done | bytes 147488 | tf_op jit(solution)/shard_map/while/body/eval_jaxpr/ppermute | solution.py:40
  171.1 1.7 collective-permute-start.7
  172.8 3.0 %collective-permute-done.7 = f32[64,288]{1,0:T(8,128)S(1)} collective-permute-done((f32[64,288]{1,0:T(8,128)S(1)}, f32[64,288]{1,0:T(8,128)S(1)}, u32[]{:S(2)}, u32[]{:S(2)}) %collective-permute-start.7) | collective-permute-done | bytes 73760 | tf_op jit(solution)/shard_map/while/body/eval_jaxpr/ppermute | solution.py:50
  175.9 3.4 %collective-permute-start.8 = (f32[64,288]{1,0:T(8,128)S(1)}, f32[64,288]{1,0:T(8,128)S(1)}, u32[]{:S(2)}, u32[]{:S(2)}) collective-permute-start(f32[64,288]{1,0:T(8,128)S(1)} %dynamic-slice_add_fusion.2), channel_id=1, source_target_pairs={{0,16},{8,24},{16,0},{24,8},{32,48},{40,56},{48,32},{56,40},{64,80... | collective-permute-start | bytes 221192 | tf_op jit(solution)/shard_map/while/body/eval_jaxpr/ppermute | solution.py:53
  179.3 2.8 %collective-permute-done.8 = f32[64,288]{1,0:T(8,128)S(1)} collective-permute-done((f32[64,288]{1,0:T(8,128)S(1)}, f32[64,288]{1,0:T(8,128)S(1)}, u32[]{:S(2)}, u32[]{:S(2)}) %collective-permute-start.8) | collective-permute-done | bytes 73760 | tf_op jit(solution)/shard_map/while/body/eval_jaxpr/ppermute | solution.py:53
  182.1 1.2 collective-permute-start.9
  183.2 3.5 %collective-permute-done.9 = f32[64,288]{1,0:T(8,128)S(1)} collective-permute-done((f32[64,288]{1,0:T(8,128)S(1)}, f32[64,288]{1,0:T(8,128)S(1)}, u32[]{:S(2)}, u32[]{:S(2)}) %collective-permute-start.9) | collective-permute-done | bytes 73760 | tf_op jit(solution)/shard_map/while/body/eval_jaxpr/ppermute | solution.py:53
  186.8 3.3 %collective-permute-start.10 = (f32[64,288]{1,0:T(8,128)S(1)}, f32[64,288]{1,0:T(8,128)S(1)}, u32[]{:S(2)}, u32[]{:S(2)}) collective-permute-start(f32[64,288]{1,0:T(8,128)S(1)} %add.511), channel_id=1, source_target_pairs={{0,64},{8,72},{16,80},{24,88},{32,96},{40,104},{48,112},{56,120},{... | collective-permute-start | bytes 221192 | tf_op jit(solution)/shard_map/while/body/eval_jaxpr/ppermute | solution.py:53
  190.1 3.6 %collective-permute-done.10 = f32[64,288]{1,0:T(8,128)S(1)} collective-permute-done((f32[64,288]{1,0:T(8,128)S(1)}, f32[64,288]{1,0:T(8,128)S(1)}, u32[]{:S(2)}, u32[]{:S(2)}) %collective-permute-start.10) | collective-permute-done | bytes 73760 | tf_op jit(solution)/shard_map/while/body/eval_jaxpr/ppermute | solution.py:53
  193.7 8.3 %collective-permute-start.11 = (f32[64,288]{1,0:T(8,128)S(1)}, f32[64,288]{1,0:T(8,128)S(1)}, u32[]{:S(2)}, u32[]{:S(2)}) collective-permute-start(f32[64,288]{1,0:T(8,128)S(1)} %add.512), channel_id=1, source_target_pairs={{0,128},{8,136},{16,144},{24,152},{32,160},{40,168},{48,176},{56,1... | collective-permute-start | bytes 221192 | tf_op jit(solution)/shard_map/while/body/eval_jaxpr/ppermute | solution.py:53
  202.1 2.6 %collective-permute-done.11 = f32[64,288]{1,0:T(8,128)S(1)} collective-permute-done((f32[64,288]{1,0:T(8,128)S(1)}, f32[64,288]{1,0:T(8,128)S(1)}, u32[]{:S(2)}, u32[]{:S(2)}) %collective-permute-start.11) | collective-permute-done | bytes 73760 | tf_op jit(solution)/shard_map/while/body/eval_jaxpr/ppermute | solution.py:53
  204.7 1.4 collective-permute-start.12
  206.1 3.3 %collective-permute-done.12 = f32[64,288]{1,0:T(8,128)S(1)} collective-permute-done((f32[64,288]{1,0:T(8,128)S(1)}, f32[64,288]{1,0:T(8,128)S(1)}, u32[]{:S(2)}, u32[]{:S(2)}) %collective-permute-start.12) | collective-permute-done | bytes 73760 | tf_op jit(solution)/shard_map/while/body/eval_jaxpr/ppermute | solution.py:55
  209.9 1.2 collective-permute-done.13
  211.2 2.0 collective-permute-start.14
  213.1 3.8 %collective-permute-done.14 = bf16[64,1024]{1,0:T(8,128)(2,1)S(1)} collective-permute-done((bf16[64,1024]{1,0:T(8,128)(2,1)S(1)}, bf16[64,1024]{1,0:T(8,128)(2,1)S(1)}, u32[]{:S(2)}, u32[]{:S(2)}) %collective-permute-start.14) | collective-permute-done | bytes 131104 | tf_op jit(solution)/shard_map/while/body/eval_jaxpr/ppermute | solution.py:63
  217.0 4.3 %collective-permute-start.15 = (bf16[64,2048]{1,0:T(8,128)(2,1)S(1)}, bf16[64,2048]{1,0:T(8,128)(2,1)S(1)}, u32[]{:S(2)}, u32[]{:S(2)}) collective-permute-start(bf16[64,2048]{1,0:T(8,128)(2,1)S(1)} %maximum_select_fusion.12), channel_id=1, source_target_pairs={{0,4},{1,5},{2,6},{3,7},{4,0},{5,1},{6,2},{7,3},{8,12},{9,13},{10,... | collective-permute-start | bytes 786440 | tf_op jit(solution)/shard_map/while/body/eval_jaxpr/ppermute | solution.py:63
  221.7 1.2 collective-permute-done.16
  222.9 0.9 collective-permute-start.17
  223.8 5.0 %collective-permute-done.17 = f32[64,64]{1,0:T(8,128)S(1)} collective-permute-done((f32[64,64]{1,0:T(8,128)S(1)}, f32[64,64]{1,0:T(8,128)S(1)}, u32[]{:S(2)}, u32[]{:S(2)}) %collective-permute-start.17) | collective-permute-done | bytes 16416 | tf_op jit(solution)/shard_map/while/body/eval_jaxpr/ppermute | solution.py:63
  228.8 6.0 %fusion.77 = f32[1024,64]{0,1:T(8,128)S(1)} fusion(f32[1024,64]{0,1:T(8,128)S(1)} %copy.24, bf16[1024,4096]{1,0:T(8,128)(2,1)} %get-tuple-element.245, bf16[64,2048]{1,0:T(8,128)(2,1)S(1)} %maximum_select_fusion.12, bf16[64,2048]{1,0:T(8,128)(2,1)S(1)} %collective-permute-done.15, pred[]{:T(512)S(6)} %eq.129), kind=kOutput, calls=%fused_computation.4.clone.1 | convolution fusion | flops 539295744 | bytes 9437185 | tf_op jit(solution)/shard_map/while/body/eval_jaxpr/dot_general | solution.py:124
  235.3 0.6 copy-done
  (69 shorter events, 6.2 us)
Async XLA Ops:
  24.2 29.7 %copy-start.1 = (f32[64,512]{1,0:T(8,128)S(1)}, f32[64,512]{1,0:T(8,128)}, u32[]{:S(2)}) copy-start(f32[64,512]{1,0:T(8,128)} %param.11) | copy-start | bytes 393220
  24.2 29.7 %copy-start.3 = (f32[1024,64]{0,1:T(8,128)S(1)}, f32[1024,64]{0,1:T(8,128)}, u32[]{:S(2)}) copy-start(f32[1024,64]{0,1:T(8,128)} %param.10) | copy-start | bytes 786436
  59.5 5.6 %collective-permute-start = (f32[64,576]{1,0:T(8,128)S(1)}, f32[64,576]{1,0:T(8,128)S(1)}, u32[]{:S(2)}, u32[]{:S(2)}) collective-permute-start(f32[64,576]{1,0:T(8,128)S(1)} %get-tuple-element.190), channel_id=1, source_target_pairs={{0,7},{1,0},{2,1},{3,2},{4,3},{5,4},{6,5},{7,6},{8,15},{9,8},{10,9... | collective-permute-start | bytes 442376 | tf_op jit(solution)/shard_map/while/body/eval_jaxpr/ppermute | solution.py:40
  59.5 9.9 %collective-permute-start.1 = (f32[64,576]{1,0:T(8,128)S(1)}, f32[64,576]{1,0:T(8,128)S(1)}, u32[]{:S(2)}, u32[]{:S(2)}) collective-permute-start(f32[64,576]{1,0:T(8,128)S(1)} %get-tuple-element.191), channel_id=1, source_target_pairs={{0,6},{1,7},{2,0},{3,1},{4,2},{5,3},{6,4},{7,5},{8,14},{9,15},{10,... | collective-permute-start | bytes 442376 | tf_op jit(solution)/shard_map/while/body/eval_jaxpr/ppermute | solution.py:40
  60.0 9.6 %collective-permute-start.2 = (f32[64,576]{1,0:T(8,128)S(1)}, f32[64,576]{1,0:T(8,128)S(1)}, u32[]{:S(2)}, u32[]{:S(2)}) collective-permute-start(f32[64,576]{1,0:T(8,128)S(1)} %get-tuple-element.192), channel_id=1, source_target_pairs={{0,5},{1,6},{2,7},{3,0},{4,1},{5,2},{6,3},{7,4},{8,13},{9,14},{10,... | collective-permute-start | bytes 442376 | tf_op jit(solution)/shard_map/while/body/eval_jaxpr/ppermute | solution.py:40
  62.7 8.6 %collective-permute-start.3 = (f32[64,576]{1,0:T(8,128)S(1)}, f32[64,576]{1,0:T(8,128)S(1)}, u32[]{:S(2)}, u32[]{:S(2)}) collective-permute-start(f32[64,576]{1,0:T(8,128)S(1)} %get-tuple-element.193), channel_id=1, source_target_pairs={{0,4},{1,5},{2,6},{3,7},{4,0},{5,1},{6,2},{7,3},{8,12},{9,13},{10,... | collective-permute-start | bytes 442376 | tf_op jit(solution)/shard_map/while/body/eval_jaxpr/ppermute | solution.py:40
  63.3 10.9 %collective-permute-start.4 = (f32[64,576]{1,0:T(8,128)S(1)}, f32[64,576]{1,0:T(8,128)S(1)}, u32[]{:S(2)}, u32[]{:S(2)}) collective-permute-start(f32[64,576]{1,0:T(8,128)S(1)} %get-tuple-element.194), channel_id=1, source_target_pairs={{0,3},{1,4},{2,5},{3,6},{4,7},{5,0},{6,1},{7,2},{8,11},{9,12},{10,... | collective-permute-start | bytes 442376 | tf_op jit(solution)/shard_map/while/body/eval_jaxpr/ppermute | solution.py:40
  65.1 14.1 %collective-permute-start.5 = (f32[64,576]{1,0:T(8,128)S(1)}, f32[64,576]{1,0:T(8,128)S(1)}, u32[]{:S(2)}, u32[]{:S(2)}) collective-permute-start(f32[64,576]{1,0:T(8,128)S(1)} %get-tuple-element.195), channel_id=1, source_target_pairs={{0,2},{1,3},{2,4},{3,5},{4,6},{5,7},{6,0},{7,1},{8,10},{9,11},{10,... | collective-permute-start | bytes 442376 | tf_op jit(solution)/shard_map/while/body/eval_jaxpr/ppermute | solution.py:40
  69.4 9.9 %collective-permute-start.6 = (f32[64,576]{1,0:T(8,128)S(1)}, f32[64,576]{1,0:T(8,128)S(1)}, u32[]{:S(2)}, u32[]{:S(2)}) collective-permute-start(f32[64,576]{1,0:T(8,128)S(1)} %get-tuple-element.196), channel_id=1, source_target_pairs={{0,1},{1,2},{2,3},{3,4},{4,5},{5,6},{6,7},{7,0},{8,9},{9,10},{10,1... | collective-permute-start | bytes 442376 | tf_op jit(solution)/shard_map/while/body/eval_jaxpr/ppermute | solution.py:40
  79.5 4.7 %collective-permute-start.7 = (f32[64,288]{1,0:T(8,128)S(1)}, f32[64,288]{1,0:T(8,128)S(1)}, u32[]{:S(2)}, u32[]{:S(2)}) collective-permute-start(f32[64,288]{1,0:T(8,128)S(1)} %constant_dynamic-slice_fusion.12), channel_id=1, source_target_pairs={{0,8},{8,0},{16,24},{24,16},{32,40},{40,32},{48,56},{56,48},{64,72... | collective-permute-start | bytes 221192 | tf_op jit(solution)/shard_map/while/body/eval_jaxpr/ppermute | solution.py:50
  84.3 7.1 %collective-permute-start.8 = (f32[64,288]{1,0:T(8,128)S(1)}, f32[64,288]{1,0:T(8,128)S(1)}, u32[]{:S(2)}, u32[]{:S(2)}) collective-permute-start(f32[64,288]{1,0:T(8,128)S(1)} %dynamic-slice_add_fusion.2), channel_id=1, source_target_pairs={{0,16},{8,24},{16,0},{24,8},{32,48},{40,56},{48,32},{56,40},{64,80... | collective-permute-start | bytes 221192 | tf_op jit(solution)/shard_map/while/body/eval_jaxpr/ppermute | solution.py:53
  91.5 4.8 %collective-permute-start.9 = (f32[64,288]{1,0:T(8,128)S(1)}, f32[64,288]{1,0:T(8,128)S(1)}, u32[]{:S(2)}, u32[]{:S(2)}) collective-permute-start(f32[64,288]{1,0:T(8,128)S(1)} %add.510), channel_id=1, source_target_pairs={{0,32},{8,40},{16,48},{24,56},{32,0},{40,8},{48,16},{56,24},{64,96... | collective-permute-start | bytes 221192 | tf_op jit(solution)/shard_map/while/body/eval_jaxpr/ppermute | solution.py:53
  96.3 7.7 %collective-permute-start.10 = (f32[64,288]{1,0:T(8,128)S(1)}, f32[64,288]{1,0:T(8,128)S(1)}, u32[]{:S(2)}, u32[]{:S(2)}) collective-permute-start(f32[64,288]{1,0:T(8,128)S(1)} %add.511), channel_id=1, source_target_pairs={{0,64},{8,72},{16,80},{24,88},{32,96},{40,104},{48,112},{56,120},{... | collective-permute-start | bytes 221192 | tf_op jit(solution)/shard_map/while/body/eval_jaxpr/ppermute | solution.py:53
  104.0 10.0 %collective-permute-start.11 = (f32[64,288]{1,0:T(8,128)S(1)}, f32[64,288]{1,0:T(8,128)S(1)}, u32[]{:S(2)}, u32[]{:S(2)}) collective-permute-start(f32[64,288]{1,0:T(8,128)S(1)} %add.512), channel_id=1, source_target_pairs={{0,128},{8,136},{16,144},{24,152},{32,160},{40,168},{48,176},{56,1... | collective-permute-start | bytes 221192 | tf_op jit(solution)/shard_map/while/body/eval_jaxpr/ppermute | solution.py:53
  114.0 4.7 %collective-permute-start.12 = (f32[64,288]{1,0:T(8,128)S(1)}, f32[64,288]{1,0:T(8,128)S(1)}, u32[]{:S(2)}, u32[]{:S(2)}) collective-permute-start(f32[64,288]{1,0:T(8,128)S(1)} %add.513), channel_id=1, source_target_pairs={{0,8},{8,0},{16,24},{24,16},{32,40},{40,32},{48,56},{56,48},{64,72... | collective-permute-start | bytes 221192 | tf_op jit(solution)/shard_map/while/body/eval_jaxpr/ppermute | solution.py:55
  119.1 1.3 collective-permute-start.13
  120.4 7.6 %collective-permute-start.14 = (bf16[64,1024]{1,0:T(8,128)(2,1)S(1)}, bf16[64,1024]{1,0:T(8,128)(2,1)S(1)}, u32[]{:S(2)}, u32[]{:S(2)}) collective-permute-start(bf16[64,1024]{1,0:T(8,128)(2,1)S(1)} %maximum_select_fusion.11), channel_id=1, source_target_pairs={{0,2},{1,3},{2,0},{3,1},{4,6},{5,7},{6,4},{7,5},{8,10},{9,11},{10,... | collective-permute-start | bytes 393224 | tf_op jit(solution)/shard_map/while/body/eval_jaxpr/ppermute | solution.py:63
  128.1 11.0 %collective-permute-start.15 = (bf16[64,2048]{1,0:T(8,128)(2,1)S(1)}, bf16[64,2048]{1,0:T(8,128)(2,1)S(1)}, u32[]{:S(2)}, u32[]{:S(2)}) collective-permute-start(bf16[64,2048]{1,0:T(8,128)(2,1)S(1)} %maximum_select_fusion.12), channel_id=1, source_target_pairs={{0,4},{1,5},{2,6},{3,7},{4,0},{5,1},{6,2},{7,3},{8,12},{9,13},{10,... | collective-permute-start | bytes 786440 | tf_op jit(solution)/shard_map/while/body/eval_jaxpr/ppermute | solution.py:63
  129.9 1.3 collective-permute-start.16
  131.2 5.9 %collective-permute-start.17 = (f32[64,64]{1,0:T(8,128)S(1)}, f32[64,64]{1,0:T(8,128)S(1)}, u32[]{:S(2)}, u32[]{:S(2)}) collective-permute-start(f32[64,64]{1,0:T(8,128)S(1)} %add.517), channel_id=1, source_target_pairs={{0,2},{1,3},{2,0},{3,1},{4,6},{5,7},{6,4},{7,5},{8,10},{9,11},{10,... | collective-permute-start | bytes 49160 | tf_op jit(solution)/shard_map/while/body/eval_jaxpr/ppermute | solution.py:63
  137.1 8.1 %collective-permute-start.18 = (f32[64,64]{1,0:T(8,128)S(1)}, f32[64,64]{1,0:T(8,128)S(1)}, u32[]{:S(2)}, u32[]{:S(2)}) collective-permute-start(f32[64,64]{1,0:T(8,128)S(1)} %add.518), channel_id=1, source_target_pairs={{0,4},{1,5},{2,6},{3,7},{4,0},{5,1},{6,2},{7,3},{8,12},{9,13},{10,... | collective-permute-start | bytes 49160 | tf_op jit(solution)/shard_map/while/body/eval_jaxpr/ppermute | solution.py:63
  151.3 6.1 %collective-permute-start = (f32[64,576]{1,0:T(8,128)S(1)}, f32[64,576]{1,0:T(8,128)S(1)}, u32[]{:S(2)}, u32[]{:S(2)}) collective-permute-start(f32[64,576]{1,0:T(8,128)S(1)} %get-tuple-element.190), channel_id=1, source_target_pairs={{0,7},{1,0},{2,1},{3,2},{4,3},{5,4},{6,5},{7,6},{8,15},{9,8},{10,9... | collective-permute-start | bytes 442376 | tf_op jit(solution)/shard_map/while/body/eval_jaxpr/ppermute | solution.py:40
  151.3 10.4 %collective-permute-start.1 = (f32[64,576]{1,0:T(8,128)S(1)}, f32[64,576]{1,0:T(8,128)S(1)}, u32[]{:S(2)}, u32[]{:S(2)}) collective-permute-start(f32[64,576]{1,0:T(8,128)S(1)} %get-tuple-element.191), channel_id=1, source_target_pairs={{0,6},{1,7},{2,0},{3,1},{4,2},{5,3},{6,4},{7,5},{8,14},{9,15},{10,... | collective-permute-start | bytes 442376 | tf_op jit(solution)/shard_map/while/body/eval_jaxpr/ppermute | solution.py:40
  151.7 10.0 %collective-permute-start.2 = (f32[64,576]{1,0:T(8,128)S(1)}, f32[64,576]{1,0:T(8,128)S(1)}, u32[]{:S(2)}, u32[]{:S(2)}) collective-permute-start(f32[64,576]{1,0:T(8,128)S(1)} %get-tuple-element.192), channel_id=1, source_target_pairs={{0,5},{1,6},{2,7},{3,0},{4,1},{5,2},{6,3},{7,4},{8,13},{9,14},{10,... | collective-permute-start | bytes 442376 | tf_op jit(solution)/shard_map/while/body/eval_jaxpr/ppermute | solution.py:40
  155.1 8.7 %collective-permute-start.3 = (f32[64,576]{1,0:T(8,128)S(1)}, f32[64,576]{1,0:T(8,128)S(1)}, u32[]{:S(2)}, u32[]{:S(2)}) collective-permute-start(f32[64,576]{1,0:T(8,128)S(1)} %get-tuple-element.193), channel_id=1, source_target_pairs={{0,4},{1,5},{2,6},{3,7},{4,0},{5,1},{6,2},{7,3},{8,12},{9,13},{10,... | collective-permute-start | bytes 442376 | tf_op jit(solution)/shard_map/while/body/eval_jaxpr/ppermute | solution.py:40
  155.3 11.1 %collective-permute-start.4 = (f32[64,576]{1,0:T(8,128)S(1)}, f32[64,576]{1,0:T(8,128)S(1)}, u32[]{:S(2)}, u32[]{:S(2)}) collective-permute-start(f32[64,576]{1,0:T(8,128)S(1)} %get-tuple-element.194), channel_id=1, source_target_pairs={{0,3},{1,4},{2,5},{3,6},{4,7},{5,0},{6,1},{7,2},{8,11},{9,12},{10,... | collective-permute-start | bytes 442376 | tf_op jit(solution)/shard_map/while/body/eval_jaxpr/ppermute | solution.py:40
  157.4 13.4 %collective-permute-start.5 = (f32[64,576]{1,0:T(8,128)S(1)}, f32[64,576]{1,0:T(8,128)S(1)}, u32[]{:S(2)}, u32[]{:S(2)}) collective-permute-start(f32[64,576]{1,0:T(8,128)S(1)} %get-tuple-element.195), channel_id=1, source_target_pairs={{0,2},{1,3},{2,4},{3,5},{4,6},{5,7},{6,0},{7,1},{8,10},{9,11},{10,... | collective-permute-start | bytes 442376 | tf_op jit(solution)/shard_map/while/body/eval_jaxpr/ppermute | solution.py:40
  161.7 9.2 %collective-permute-start.6 = (f32[64,576]{1,0:T(8,128)S(1)}, f32[64,576]{1,0:T(8,128)S(1)}, u32[]{:S(2)}, u32[]{:S(2)}) collective-permute-start(f32[64,576]{1,0:T(8,128)S(1)} %get-tuple-element.196), channel_id=1, source_target_pairs={{0,1},{1,2},{2,3},{3,4},{4,5},{5,6},{6,7},{7,0},{8,9},{9,10},{10,1... | collective-permute-start | bytes 442376 | tf_op jit(solution)/shard_map/while/body/eval_jaxpr/ppermute | solution.py:40
  171.1 4.7 %collective-permute-start.7 = (f32[64,288]{1,0:T(8,128)S(1)}, f32[64,288]{1,0:T(8,128)S(1)}, u32[]{:S(2)}, u32[]{:S(2)}) collective-permute-start(f32[64,288]{1,0:T(8,128)S(1)} %constant_dynamic-slice_fusion.12), channel_id=1, source_target_pairs={{0,8},{8,0},{16,24},{24,16},{32,40},{40,32},{48,56},{56,48},{64,72... | collective-permute-start | bytes 221192 | tf_op jit(solution)/shard_map/while/body/eval_jaxpr/ppermute | solution.py:50
  175.9 6.2 %collective-permute-start.8 = (f32[64,288]{1,0:T(8,128)S(1)}, f32[64,288]{1,0:T(8,128)S(1)}, u32[]{:S(2)}, u32[]{:S(2)}) collective-permute-start(f32[64,288]{1,0:T(8,128)S(1)} %dynamic-slice_add_fusion.2), channel_id=1, source_target_pairs={{0,16},{8,24},{16,0},{24,8},{32,48},{40,56},{48,32},{56,40},{64,80... | collective-permute-start | bytes 221192 | tf_op jit(solution)/shard_map/while/body/eval_jaxpr/ppermute | solution.py:53
  182.1 4.7 %collective-permute-start.9 = (f32[64,288]{1,0:T(8,128)S(1)}, f32[64,288]{1,0:T(8,128)S(1)}, u32[]{:S(2)}, u32[]{:S(2)}) collective-permute-start(f32[64,288]{1,0:T(8,128)S(1)} %add.510), channel_id=1, source_target_pairs={{0,32},{8,40},{16,48},{24,56},{32,0},{40,8},{48,16},{56,24},{64,96... | collective-permute-start | bytes 221192 | tf_op jit(solution)/shard_map/while/body/eval_jaxpr/ppermute | solution.py:53
  186.8 6.9 %collective-permute-start.10 = (f32[64,288]{1,0:T(8,128)S(1)}, f32[64,288]{1,0:T(8,128)S(1)}, u32[]{:S(2)}, u32[]{:S(2)}) collective-permute-start(f32[64,288]{1,0:T(8,128)S(1)} %add.511), channel_id=1, source_target_pairs={{0,64},{8,72},{16,80},{24,88},{32,96},{40,104},{48,112},{56,120},{... | collective-permute-start | bytes 221192 | tf_op jit(solution)/shard_map/while/body/eval_jaxpr/ppermute | solution.py:53
  193.7 10.9 %collective-permute-start.11 = (f32[64,288]{1,0:T(8,128)S(1)}, f32[64,288]{1,0:T(8,128)S(1)}, u32[]{:S(2)}, u32[]{:S(2)}) collective-permute-start(f32[64,288]{1,0:T(8,128)S(1)} %add.512), channel_id=1, source_target_pairs={{0,128},{8,136},{16,144},{24,152},{32,160},{40,168},{48,176},{56,1... | collective-permute-start | bytes 221192 | tf_op jit(solution)/shard_map/while/body/eval_jaxpr/ppermute | solution.py:53
  204.7 4.7 %collective-permute-start.12 = (f32[64,288]{1,0:T(8,128)S(1)}, f32[64,288]{1,0:T(8,128)S(1)}, u32[]{:S(2)}, u32[]{:S(2)}) collective-permute-start(f32[64,288]{1,0:T(8,128)S(1)} %add.513), channel_id=1, source_target_pairs={{0,8},{8,0},{16,24},{24,16},{32,40},{40,32},{48,56},{56,48},{64,72... | collective-permute-start | bytes 221192 | tf_op jit(solution)/shard_map/while/body/eval_jaxpr/ppermute | solution.py:55
  209.8 1.3 collective-permute-start.13
  211.2 5.8 %collective-permute-start.14 = (bf16[64,1024]{1,0:T(8,128)(2,1)S(1)}, bf16[64,1024]{1,0:T(8,128)(2,1)S(1)}, u32[]{:S(2)}, u32[]{:S(2)}) collective-permute-start(bf16[64,1024]{1,0:T(8,128)(2,1)S(1)} %maximum_select_fusion.11), channel_id=1, source_target_pairs={{0,2},{1,3},{2,0},{3,1},{4,6},{5,7},{6,4},{7,5},{8,10},{9,11},{10,... | collective-permute-start | bytes 393224 | tf_op jit(solution)/shard_map/while/body/eval_jaxpr/ppermute | solution.py:63
  217.0 11.8 %collective-permute-start.15 = (bf16[64,2048]{1,0:T(8,128)(2,1)S(1)}, bf16[64,2048]{1,0:T(8,128)(2,1)S(1)}, u32[]{:S(2)}, u32[]{:S(2)}) collective-permute-start(bf16[64,2048]{1,0:T(8,128)(2,1)S(1)} %maximum_select_fusion.12), channel_id=1, source_target_pairs={{0,4},{1,5},{2,6},{3,7},{4,0},{5,1},{6,2},{7,3},{8,12},{9,13},{10,... | collective-permute-start | bytes 786440 | tf_op jit(solution)/shard_map/while/body/eval_jaxpr/ppermute | solution.py:63
  221.6 1.3 collective-permute-start.16
  222.9 5.9 %collective-permute-start.17 = (f32[64,64]{1,0:T(8,128)S(1)}, f32[64,64]{1,0:T(8,128)S(1)}, u32[]{:S(2)}, u32[]{:S(2)}) collective-permute-start(f32[64,64]{1,0:T(8,128)S(1)} %add.517), channel_id=1, source_target_pairs={{0,2},{1,3},{2,0},{3,1},{4,6},{5,7},{6,4},{7,5},{8,10},{9,11},{10,... | collective-permute-start | bytes 49160 | tf_op jit(solution)/shard_map/while/body/eval_jaxpr/ppermute | solution.py:63
  228.8 6.1 %collective-permute-start.18 = (f32[64,64]{1,0:T(8,128)S(1)}, f32[64,64]{1,0:T(8,128)S(1)}, u32[]{:S(2)}, u32[]{:S(2)}) collective-permute-start(f32[64,64]{1,0:T(8,128)S(1)} %add.518), channel_id=1, source_target_pairs={{0,4},{1,5},{2,6},{3,7},{4,0},{5,1},{6,2},{7,3},{8,12},{9,13},{10,... | collective-permute-start | bytes 49160 | tf_op jit(solution)/shard_map/while/body/eval_jaxpr/ppermute | solution.py:63
  235.3 0.7 copy-start
  235.3 0.7 copy-start.2
